TPU v7x, 256 devices: a whole 4x4x8 slice. The times are simulated.
256 devices in a mesh: mem: 32 (over z, x), pipe: 4 (over y), dp: 2 (over core).
Axes of the slice: x: 4, y: 4, z: 8, core: 2. Of those that a mesh axis runs over, the one named last changes fastest.
Arguments:
- values: bfloat16 [32768, 4096], P(('dp', 'mem'), 'pipe'), parts along dimension 0, may hold values from -6 to 6
- cotangent: bfloat16 [8192, 4096], P(('dp', 'mem'), 'pipe'), parts along dimension 0, may hold values from -6 to 6
- scores: float32 [8192, 4, 32], P(('dp', 'mem')), parts along dimension 0, may hold values from -8 to 410, as said below
- row_lists: int32 [64, 32, 128], P(('dp', 'mem')), parts along dimension 0, may hold values from -1 to 511, as said below
- sel_slot: int32 [8192, 4, 32], P(('dp', 'mem')), parts along dimension 0, may hold values from 0 to 4095, as said below
Outputs:
- mem_out: bfloat16 [8192, 4096], P(('dp', 'mem'), 'pipe'), parts along dimension 0
- grad_values: bfloat16 [32768, 4096], P(('dp', 'mem'), 'pipe'), parts along dimension 0
- grad_scores: float32 [8192, 4, 32], P(('dp', 'mem')), parts along dimension 0
There are 2 independent parts, one for each index of `dp`. A program takes and returns all parts, laid end to end along the dimension named above; each array names one. Nothing has to cross between parts.
Inputs may be any that keep to these rules, and one draw needn't show every extreme that they name: `row_lists`: each entry is a row of the owner's shard, or -1 for an empty slot; the rows of one block are distinct and its empty slots come last; in every draw some owner receives full blocks of 128 rows from every device. `sel_slot`: each entry names a slot of the request blocks of the token's own mem index, and that slot holds a row; the 32 entries of one token and head are distinct. `scores`: scores are finite.
All inputs are finite; a program needn't handle non-finite values.
Results may differ from a plain program's by a relative error of at most 0.013.
Values may be sent and summed in bfloat16 or wider, within the bound.
No kernel may reach another device: no remote copies, remote signals or barrier semaphores. Data moves between devices by JAX's collectives and lax.ppermute only.
A program may use at most 128 MiB of HBM per device.

v0:
```python
import jax
import jax.numpy as jnp
from jax import lax
from jax.sharding import PartitionSpec as P


def body(values, cotangent, scores, row_lists, sel_slot):
    owners = lax.axis_size("mem")
    tokens_here = cotangent.shape[0]
    cap_slots = row_lists.shape[2]
    slot_count = owners * cap_slots
    width = values.shape[1]
    table_rows = values.shape[0]
    highest = lax.Precision.HIGHEST
    all_cot = lax.all_gather(cotangent, "mem", axis=0, tiled=True)
    weights = jax.nn.softmax(scores, axis=-1)
    chosen = sel_slot.reshape(tokens_here, -1)
    owner_of = chosen // cap_slots
    place_of = chosen % cap_slots
    owner_hot = (owner_of[..., None] == jnp.arange(owners, dtype=jnp.int32)[None, None, :]).astype(
        jnp.float32
    )
    place_hot = (
        place_of[..., None] == jnp.arange(cap_slots, dtype=jnp.int32)[None, None, :]
    ).astype(jnp.float32)
    weighted_owner = owner_hot * weights.reshape(tokens_here, -1)[..., None]
    combined = jnp.einsum(
        "tpo,tpc->toc",
        weighted_owner,
        place_hot,
        precision=highest,
        preferred_element_type=jnp.float32,
    ).astype(jnp.bfloat16)
    asked = lax.all_to_all(row_lists[0], "mem", split_axis=0, concat_axis=0, tiled=True)
    asked = asked.reshape(owners, cap_slots)
    row_hot = (asked[..., None] == jnp.arange(table_rows, dtype=jnp.int32)).astype(jnp.bfloat16)
    looked = jnp.dot(
        row_hot.reshape(slot_count, table_rows), values, preferred_element_type=jnp.float32
    ).astype(jnp.bfloat16)
    replied = lax.all_to_all(
        looked.reshape(owners, cap_slots, width), "mem", 0, 0, tiled=True
    )
    gathered_rows = replied.reshape(slot_count, width)
    flat_comb = combined.reshape(tokens_here, slot_count)
    mem_out = jnp.dot(flat_comb, gathered_rows, preferred_element_type=jnp.float32).astype(
        jnp.bfloat16
    )
    products = lax.dot_general(
        cotangent, gathered_rows, (((1,), (1,)), ((), ())), preferred_element_type=jnp.float32
    )
    products = products.reshape(tokens_here, owners, cap_slots)
    picked = jnp.einsum(
        "tpc,toc->tpo", place_hot, products, precision=highest, preferred_element_type=jnp.float32
    )
    partial_dots = jnp.sum(picked * owner_hot, axis=-1).reshape(weights.shape)
    full_dots = lax.psum(partial_dots.astype(jnp.bfloat16), "pipe").astype(jnp.float32)
    grad_scores = weights * (full_dots - jnp.sum(weights * full_dots, axis=-1, keepdims=True))
    comb_in = lax.all_to_all(jnp.swapaxes(combined, 0, 1), "mem", 0, 0, tiled=True)
    comb_in = comb_in.reshape(owners, tokens_here, cap_slots)
    in_rows = jnp.einsum("stc,scr->str", comb_in, row_hot, preferred_element_type=jnp.float32)
    in_rows = in_rows.astype(jnp.bfloat16)
    grad_full = lax.dot_general(
        in_rows.reshape(slot_count, table_rows),
        all_cot,
        (((0,), (0,)), ((), ())),
        preferred_element_type=jnp.float32,
    )
    grad_values = grad_full.astype(jnp.bfloat16)
    return (mem_out, grad_values, grad_scores)


def solution(mesh):
    placed = (
        P(("dp", "mem"), "pipe"),
        P(("dp", "mem"), "pipe"),
        P(("dp", "mem"), None, None),
        P(("dp", "mem"), None, None),
        P(("dp", "mem"), None, None),
    )
    return jax.shard_map(
        body,
        mesh=mesh,
        in_specs=placed,
        out_specs=(
            P(("dp", "mem"), "pipe"),
            P(("dp", "mem"), "pipe"),
            P(("dp", "mem"), None, None),
        ),
        check_vma=False,
    )
```

profile of v0, /device:TPU:6, one launch (start us, length us, event | category | flops | bytes accessed | tf_op | source)
XLA Modules:
  0.0 344.9 jit_solution(16141070091280785732)
XLA Ops:
  7.2 0.0 copy-start
  7.2 11.7 %all-to-all-start = ((s32[32,1,128]{2,1,0:T(1,128)}), s32[32,1,128]{2,1,0:T(1,128)S(1)}, u32[]{:S(2)}, u32[]{:S(2)}) async-start(s32[32,1,128]{2,1,0:T(1,128)} %bitcast.35), calls=%async_computation | async-start | bytes 32768 | tf_op jit(solution)/shard_map/all_to_all | solution.py:34
  18.9 0.9 copy.25
  19.8 0.1 add_select_fusion.1
  19.9 0.0 copy-start.4
  19.9 1.0 fusion.19
  20.9 0.1 copy.29
  21.0 5.9 %fusion.14 = bf16[128,32,128]{2,1,0:T(8,128)(2,1)S(1)} fusion(s32[128,128]{1,0:T(8,128)S(1)} %get-tuple-element.4, f32[128,128]{1,0:T(8,128)S(1)} %copy.29, s32[128,128]{1,0:T(8,128)S(1)} %get-tuple-element.3), kind=kOutput, calls=%fused_computation.20 | convolution fusion | flops 808976384 | bytes 1245184 | tf_op jit(solution)/shard_map/tpo,tpc->toc/dot_general | solution.py:27
  26.8 0.0 copy-start.1
  26.9 1.0 copy-done.1
  27.9 1.4 copy.31
  29.3 0.0 copy-done.4
  29.3 0.0 all-to-all-done
  29.3 9.8 %all-to-all-start.2 = ((bf16[32,128,128]{2,1,0:T(8,128)(2,1)}), bf16[32,128,128]{2,1,0:T(8,128)(2,1)S(1)}, u32[]{:S(2)}, u32[]{:S(2)}) async-start(bf16[32,128,128]{2,1,0:T(8,128)(2,1)} %copy.31), calls=%async_computation.2 | async-start | bytes 2097152 | tf_op jit(solution)/shard_map/all_to_all | solution.py:58
  39.0 0.0 all-gather.2.cloned.1.call-start
  39.1 0.7 all-gather.2.cloned.1.call-update
  39.8 0.0 copy-done
  39.8 6.8 %fusion.7 = bf16[4096,1024]{1,0:T(8,128)(2,1)} fusion(bf16[512,1024]{1,0:T(8,128)(2,1)S(1)} %copy-done, s32[4096]{0:T(1024)S(1)} %bitcast.32), kind=kOutput, calls=%fused_computation.10 | convolution fusion | flops 4301258752 | bytes 9453568 | tf_op jit(solution)/shard_map/dot_general | solution.py:37
  46.5 22.5 %all-to-all-done.2 = bf16[32,128,128]{2,1,0:T(8,128)(2,1)S(1)} async-done(((bf16[32,128,128]{2,1,0:T(8,128)(2,1)}), bf16[32,128,128]{2,1,0:T(8,128)(2,1)S(1)}, u32[]{:S(2)}, u32[]{:S(2)}) %all-to-all-start.2) | async-done | bytes 1048608 | tf_op jit(solution)/shard_map/all_to_all | solution.py:58
  69.1 5.1 %all-to-all-start.1 = ((bf16[32,128,1024]{2,1,0:T(8,128)(2,1)}), bf16[32,128,1024]{2,1,0:T(8,128)(2,1)}, u32[]{:S(2)}, u32[]{:S(2)}) async-start(bf16[32,128,1024]{2,1,0:T(8,128)(2,1)} %bitcast.27), calls=%async_computation.1 | async-start | bytes 16777216 | tf_op jit(solution)/shard_map/all_to_all | solution.py:40
  74.2 3.5 %fusion.12 = bf16[32,128,512]{2,1,0:T(8,128)(2,1)} fusion(bf16[32,128,128]{2,1,0:T(8,128)(2,1)S(1)} %all-to-all-done.2, s32[32,128]{1,0:T(8,128)S(1)} %bitcast.33), kind=kOutput, calls=%fused_computation.15 | convolution fusion | flops 541065216 | bytes 5259264 | tf_op jit(solution)/shard_map/stc,scr->str/dot_general | solution.py:60
  77.7 164.1 %all-gather.2.cloned.1.call-done = bf16[4096,1024]{1,0:T(8,128)(2,1)} async-done(((bf16[128,1024]{1,0:T(8,128)(2,1)}), bf16[4096,1024]{1,0:T(8,128)(2,1)}) %all-gather.2.cloned.1.call-update) | async-done | bytes 8388624 | tf_op jit(solution)/shard_map/all_gather | solution.py:15
  241.8 0.0 copy-start.3
  241.8 10.2 %convolution_convert_fusion = bf16[512,1024]{1,0:T(8,128)(2,1)} fusion(bf16[4096,512]{1,0:T(8,128)(2,1)} %bitcast.29, bf16[4096,1024]{1,0:T(8,128)(2,1)} %all-gather.2.cloned.1.call-done), kind=kOutput, calls=%fused_computation.19 | convolution fusion | flops 4295491584 | bytes 13631488 | tf_op jit(solution)/shard_map/dot_general | solution.py:62
  252.0 46.1 %all-to-all-done.1 = bf16[32,128,1024]{2,1,0:T(8,128)(2,1)} async-done(((bf16[32,128,1024]{2,1,0:T(8,128)(2,1)}), bf16[32,128,1024]{2,1,0:T(8,128)(2,1)}, u32[]{:S(2)}, u32[]{:S(2)}) %all-to-all-start.1) | async-done | bytes 8388640 | tf_op jit(solution)/shard_map/all_to_all | solution.py:40
  298.1 0.0 copy-done.3
  298.1 5.7 %fusion.32 = f32[4096,128]{1,0:T(8,128)S(1)} fusion(bf16[4096,1024]{1,0:T(8,128)(2,1)} %bitcast.9, bf16[128,1024]{1,0:T(8,128)(2,1)S(1)} %copy-done.3), kind=kOutput, calls=%fused_computation.44 | convolution fusion | flops 1073741824 | bytes 10747904 | tf_op jit(solution)/shard_map/dot_general | solution.py:48
  303.8 0.0 copy-start.5
  303.8 2.0 copy.32
  305.8 0.0 copy-done.5
  305.8 0.0 copy-start.2
  305.8 8.5 %select_reduce_fusion = bf16[128,128]{1,0:T(8,128)(2,1)S(1)} fusion(f32[128,32,128]{2,1,0:T(8,128)} %copy.32, s32[128,128]{1,0:T(8,128)S(1)} %copy-done.5, s32[128,128]{1,0:T(8,128)S(1)} %get-tuple-element.3), kind=kOutput, calls=%fused_computation.16 | convolution fusion | flops 808960000 | bytes 2260992 | tf_op jit(solution)/shard_map/tpc,toc->tpo/dot_general | solution.py:52
  314.3 0.1 copy.33
  314.5 17.4 %psum.7 = bf16[128,4,32]{0,2,1:T(8,128)(2,1)S(1)} all-reduce(bf16[128,4,32]{0,2,1:T(8,128)(2,1)S(1)} %bitcast.31), channel_id=1, replica_groups=mesh['mem'=32,'pipe'=4,'dp'=2] {'pipe'}, use_global_device_ids=true, to_apply=%region_3.4 | all-reduce | flops 16384 | bytes 65536 | tf_op jit(solution)/shard_map/psum | solution.py:56
  331.8 0.7 fusion.22
  332.5 0.0 copy-done.2
  332.5 5.6 %fusion.17 = bf16[128,1024]{1,0:T(8,128)(2,1)} fusion(bf16[32,128,1024]{2,1,0:T(8,128)(2,1)} %all-to-all-done.1, bf16[128,32,128]{2,1,0:T(8,128)(2,1)S(1)} %copy-done.2), kind=kOutput, calls=%fused_computation.22 | convolution fusion | flops 1073872896 | bytes 9699328 | tf_op jit(solution)/shard_map/dot_general | solution.py:45
Async XLA Ops:
  7.2 32.6 %copy-start = (bf16[512,1024]{1,0:T(8,128)(2,1)S(1)}, bf16[512,1024]{1,0:T(8,128)(2,1)}, u32[]{:S(2)}) copy-start(bf16[512,1024]{1,0:T(8,128)(2,1)} %param.5) | copy-start | bytes 3145732
  7.2 22.1 %all-to-all-start = ((s32[32,1,128]{2,1,0:T(1,128)}), s32[32,1,128]{2,1,0:T(1,128)S(1)}, u32[]{:S(2)}, u32[]{:S(2)}) async-start(s32[32,1,128]{2,1,0:T(1,128)} %bitcast.35), calls=%async_computation | async-start | bytes 32768 | tf_op jit(solution)/shard_map/all_to_all | solution.py:34
  19.9 9.4 %copy-start.4 = (s32[128,128]{1,0:T(8,128)}, s32[128,128]{1,0:T(8,128)S(1)}, u32[]{:S(2)}) copy-start(s32[128,128]{1,0:T(8,128)S(1)} %get-tuple-element.4) | copy-start | bytes 196612
  26.8 1.0 copy-start.1
  29.3 39.8 %all-to-all-start.2 = ((bf16[32,128,128]{2,1,0:T(8,128)(2,1)}), bf16[32,128,128]{2,1,0:T(8,128)(2,1)S(1)}, u32[]{:S(2)}, u32[]{:S(2)}) async-start(bf16[32,128,128]{2,1,0:T(8,128)(2,1)} %copy.31), calls=%async_computation.2 | async-start | bytes 2097152 | tf_op jit(solution)/shard_map/all_to_all | solution.py:58
  39.0 202.8 %all-gather.2.cloned.1.call-start = ((), (), s32[]{:S(2)}) async-start(), calls=%async_computation.3 | async-start | bytes 8650752 | tf_op jit(solution)/shard_map/all_gather | solution.py:15
  69.1 229.0 %all-to-all-start.1 = ((bf16[32,128,1024]{2,1,0:T(8,128)(2,1)}), bf16[32,128,1024]{2,1,0:T(8,128)(2,1)}, u32[]{:S(2)}, u32[]{:S(2)}) async-start(bf16[32,128,1024]{2,1,0:T(8,128)(2,1)} %bitcast.27), calls=%async_computation.1 | async-start | bytes 16777216 | tf_op jit(solution)/shard_map/all_to_all | solution.py:40
  241.8 56.3 %copy-start.3 = (bf16[128,1024]{1,0:T(8,128)(2,1)S(1)}, bf16[128,1024]{1,0:T(8,128)(2,1)}, u32[]{:S(2)}) copy-start(bf16[128,1024]{1,0:T(8,128)(2,1)} %param.6) | copy-start | bytes 786436
  303.8 2.0 copy-start.5
  305.8 26.7 %copy-start.2 = (bf16[128,32,128]{2,1,0:T(8,128)(2,1)S(1)}, bf16[128,32,128]{2,1,0:T(8,128)(2,1)}, u32[]{:S(2)}) copy-start(bf16[128,32,128]{2,1,0:T(8,128)(2,1)} %copy-done.1) | copy-start | bytes 3145732
Sparse Core Ops, SparseCore 0:
  42.4 199.3 all-gather.1
where the time goes:
time: 349 us; the launch traced here: 345 us
  waiting for transfers between devices  233 us (67%)
  matrix products  46.1 us (13%)
  starting transfers between devices  26.7 us (8%)
  blocking collectives  17.4 us (5%)
  between operations  14.2 us (4%)
  local copies, waits for them, and re-layouts  5.58 us (2%)
    all_gather x1, waiting for transfers between devices, body(): all_cot = lax.all_gather(cotangent, 'mem', axis=0, tiled=True)  164 us
    all_to_all x1, waiting for transfers between devices, body(): lax.all_to_all(looked.reshape(owners, cap_slots, width), 'mem', 0, 0, til...  46.1 us
    all_to_all x1, waiting for transfers between devices, body(): lax.all_to_all(jnp.swapaxes(combined, 0, 1), 'mem', 0, 0, tiled=True)  22.5 us
    psum x1, blocking collectives, body(): lax.psum(partial_dots.astype(jnp.bfloat16), 'pipe').astype(jnp.float32)  17.4 us
    all_to_all x1, starting transfers between devices, body(): lax.all_to_all(row_lists[0], 'mem', split_axis=0, concat_axis=0, tiled=True)  11.7 us
    dot_general x1, matrix products, body(): lax.dot_general(in_rows.reshape(slot_count, table_rows), all_cot, (((0,),...  10.2 us
    all_to_all x1, starting transfers between devices, body(): lax.all_to_all(jnp.swapaxes(combined, 0, 1), 'mem', 0, 0, tiled=True)  9.78 us
    dot_general x1, matrix products, body(): jnp.einsum('tpc,toc->tpo', place_hot, products, precision=highest, prefer...  8.49 us
  transfers between devices with their start and end apart: 4, of which 3 were waited for; matrix products, arithmetic and copies ran while one was open for 9% of the time, Pallas kernels for 0%

commit v1 on v0

--- a/solution.py
+++ b/solution.py
@@ -55,8 +55,25 @@
     partial_dots = jnp.sum(picked * owner_hot, axis=-1).reshape(weights.shape)
     full_dots = lax.psum(partial_dots.astype(jnp.bfloat16), "pipe").astype(jnp.float32)
     grad_scores = weights * (full_dots - jnp.sum(weights * full_dots, axis=-1, keepdims=True))
-    comb_in = lax.all_to_all(jnp.swapaxes(combined, 0, 1), "mem", 0, 0, tiled=True)
-    comb_in = comb_in.reshape(owners, tokens_here, cap_slots)
+    along_x = 4
+    along_z = owners // along_x
+    me = lax.axis_index("mem")
+    my_z, my_x = me // along_x, me % along_x
+    by_owner = jnp.swapaxes(combined, 0, 1).reshape(along_z, along_x, tokens_here, cap_slots)
+    rolled = jnp.take(by_owner, (my_x + jnp.arange(along_x)) % along_x, axis=1)
+    stage = [rolled[:, 0]]
+    for shift in range(1, along_x):
+        ring = [(i, (i // along_x) * along_x + (i + shift) % along_x) for i in range(owners)]
+        stage.append(lax.ppermute(rolled[:, shift], "mem", ring))
+    rolled = jnp.take(jnp.stack(stage, axis=1), (my_z + jnp.arange(along_z)) % along_z, axis=0)
+    got = [rolled[0]]
+    for shift in range(1, along_z):
+        ring = [(i, (i + shift * along_x) % owners) for i in range(owners)]
+        got.append(lax.ppermute(rolled[shift], "mem", ring))
+    got = jnp.stack(got)
+    from_z = (my_z - jnp.arange(along_z)) % along_z
+    from_x = (my_x - jnp.arange(along_x)) % along_x
+    comb_in = got[from_z[:, None], from_x[None, :]].reshape(owners, tokens_here, cap_slots)
     in_rows = jnp.einsum("stc,scr->str", comb_in, row_hot, preferred_element_type=jnp.float32)
     in_rows = in_rows.astype(jnp.bfloat16)
     grad_full = lax.dot_general(

time: 349 us -> 362 us (1.037)
  starting transfers between devices: 26.7 us -> 37.9 us
    ppermute x0 -> x10, waiting for transfers between devices: none -> 228 us  [the longest x7 184 us: body(): got.append(lax.ppermute(rolled[shift], 'mem', ring))]
    all_gather x1, waiting for transfers between devices: 164 us -> 0.01 us  [body(): all_cot = lax.all_gather(cotangent, 'mem', axis=0, tiled=True)]
    all_to_all x1, waiting for transfers between devices: 46.1 us -> 0.01 us  [body(): lax.all_to_all(looked.reshape(owners, cap_slots, width), 'mem', 0, 0, til...]
    all_to_all x1 -> x0, waiting for transfers between devices: 22.5 us -> none  [body(): lax.all_to_all(jnp.swapaxes(combined, 0, 1), 'mem', 0, 0, tiled=True)]
    ppermute x0 -> x10, starting transfers between devices: none -> 19.5 us  [the longest x7 15.3 us: body(): got.append(lax.ppermute(rolled[shift], 'mem', ring))]
    all_to_all x1 -> x0, starting transfers between devices: 9.78 us -> none  [body(): lax.all_to_all(jnp.swapaxes(combined, 0, 1), 'mem', 0, 0, tiled=True)]
    all_to_all x1, waiting for transfers between devices: 0.01 us -> 7.17 us  [body(): lax.all_to_all(row_lists[0], 'mem', split_axis=0, concat_axis=0, tiled=True)]
  transfers between devices with their start and end apart: 4 -> 13, of which waited for: 3 -> 6; matrix products, arithmetic and copies ran while one was open for 9% -> 9% of each run, Pallas kernels for 0% -> 0%
where the time goes in v1:
time: 362 us; the launch traced here: 361 us
  waiting for transfers between devices  236 us (65%)
  matrix products  46 us (13%)
  starting transfers between devices  37.9 us (10%)
  blocking collectives  17.3 us (5%)
  between operations  14.4 us (4%)
  local copies, waits for them, and re-layouts  7.45 us (2%)
    ppermute x7, waiting for transfers between devices, body(): got.append(lax.ppermute(rolled[shift], 'mem', ring))  184 us
    ppermute x3, waiting for transfers between devices, body(): stage.append(lax.ppermute(rolled[:, shift], 'mem', ring))  43.5 us
    psum x1, blocking collectives, body(): lax.psum(partial_dots.astype(jnp.bfloat16), 'pipe').astype(jnp.float32)  17.3 us
    ppermute x7, starting transfers between devices, body(): got.append(lax.ppermute(rolled[shift], 'mem', ring))  15.3 us
    all_to_all x1, starting transfers between devices, body(): lax.all_to_all(row_lists[0], 'mem', split_axis=0, concat_axis=0, tiled=True)  11.7 us
    dot_general x1, matrix products, body(): lax.dot_general(in_rows.reshape(slot_count, table_rows), all_cot, (((0,),...  10.2 us
    dot_general x1, matrix products, body(): jnp.einsum('tpc,toc->tpo', place_hot, products, precision=highest, prefer...  8.49 us
  transfers between devices with their start and end apart: 13, of which 6 were waited for; matrix products, arithmetic and copies ran while one was open for 9% of the time, Pallas kernels for 0%

profile of v1, /device:TPU:6, one launch (start us, length us, event | category | flops | bytes accessed | tf_op | source)
XLA Modules:
  0.0 361.1 jit_solution(9476281212096793444)
XLA Ops:
  7.2 11.7 %all-to-all-start = ((s32[32,1,128]{2,1,0:T(1,128)}), s32[32,1,128]{2,1,0:T(1,128)S(1)}, u32[]{:S(2)}, u32[]{:S(2)}) async-start(s32[32,1,128]{2,1,0:T(1,128)} %bitcast.85), calls=%async_computation | async-start | bytes 32768 | tf_op jit(solution)/shard_map/all_to_all | solution.py:34
  18.9 0.7 all-gather.2.cloned.1.call-update
  19.6 7.2 %all-to-all-done = s32[32,1,128]{2,1,0:T(1,128)S(1)} async-done(((s32[32,1,128]{2,1,0:T(1,128)}), s32[32,1,128]{2,1,0:T(1,128)S(1)}, u32[]{:S(2)}, u32[]{:S(2)}) %all-to-all-start) | async-done | bytes 16416 | tf_op jit(solution)/shard_map/all_to_all | solution.py:34
  26.8 6.7 %fusion.7 = bf16[4096,1024]{1,0:T(8,128)(2,1)} fusion(bf16[512,1024]{1,0:T(8,128)(2,1)S(1)} %copy-done, s32[4096]{0:T(1024)S(1)} %bitcast.82), kind=kOutput, calls=%fused_computation.13 | convolution fusion | flops 4301258752 | bytes 9453568 | tf_op jit(solution)/shard_map/dot_general | solution.py:37
  33.5 6.7 %all-to-all-start.1 = ((bf16[32,128,1024]{2,1,0:T(8,128)(2,1)}), bf16[32,128,1024]{2,1,0:T(8,128)(2,1)}, u32[]{:S(2)}, u32[]{:S(2)}) async-start(bf16[32,128,1024]{2,1,0:T(8,128)(2,1)} %bitcast.74), calls=%async_computation.1 | async-start | bytes 16777216 | tf_op jit(solution)/shard_map/all_to_all | solution.py:40
  40.2 1.0 fusion.19
  41.2 0.1 copy.48
  41.3 0.1 copy.44
  41.4 0.1 add_select_fusion.1
  41.5 5.9 %fusion.14 = bf16[128,32,128]{2,1,0:T(8,128)(2,1)S(1)} fusion(s32[128,128]{1,0:T(8,128)S(1)} %get-tuple-element.16, f32[128,128]{1,0:T(8,128)S(1)} %copy.48, s32[128,128]{1,0:T(8,128)S(1)} %get-tuple-element.15), kind=kOutput, calls=%fused_computation.23 | convolution fusion | flops 808976384 | bytes 1245184 | tf_op jit(solution)/shard_map/tpo,tpc->toc/dot_general | solution.py:27
  47.4 1.1 copy-done.1
  48.4 0.4 copy.50
  48.9 0.7 gather_fusion
  49.7 0.2 select_bitcast_fusion
  49.9 0.1 fusion.44
  49.9 0.9 collective-permute-start.2
  50.9 1.0 collective-permute-start.1
  51.9 2.2 collective-permute-start
  54.2 30.3 %collective-permute-done.2 = bf16[8,128,128]{2,1,0:T(8,128)(2,1)S(1)} collective-permute-done((bf16[8,128,128]{2,1,0:T(8,128)(2,1)S(1)}, bf16[8,128,128]{2,1,0:T(8,128)(2,1)S(1)}, u32[]{:S(2)}, u32[]{:S(2)}) %collective-permute-start.2) | collective-permute-done | bytes 262176 | tf_op jit(solution)/shard_map/ppermute | solution.py:67
  84.4 13.2 %collective-permute-done.1 = bf16[8,128,128]{2,1,0:T(8,128)(2,1)S(1)} collective-permute-done((bf16[8,128,128]{2,1,0:T(8,128)(2,1)S(1)}, bf16[8,128,128]{2,1,0:T(8,128)(2,1)S(1)}, u32[]{:S(2)}, u32[]{:S(2)}) %collective-permute-start.1) | collective-permute-done | bytes 262176 | tf_op jit(solution)/shard_map/ppermute | solution.py:67
  97.6 0.1 pad_maximum_fusion
  97.8 0.1 copy.51
  97.9 0.8 gather_fusion.1
  98.6 0.2 broadcast_select_fusion
  98.8 0.1 slice_bitcast_fusion.3
  98.9 0.1 collective-permute-start.3
  99.0 0.1 broadcast_or_fusion
  99.1 0.1 reshape.254
  99.2 5.4 %collective-permute-start.9 = (bf16[4,128,128]{2,1,0:T(8,128)(2,1)S(1)}, bf16[4,128,128]{2,1,0:T(8,128)(2,1)S(1)}, u32[]{:S(2)}, u32[]{:S(2)}) collective-permute-start(bf16[4,128,128]{2,1,0:T(8,128)(2,1)S(1)} %get-tuple-element.3), channel_id=1, source_target_pairs={{0,224},{8,232},{16,240},{24,248},{32,0},{40,8},{48,16},{56,24},{6... | collective-permute-start | bytes 393224 | tf_op jit(solution)/shard_map/ppermute | solution.py:72
  104.6 1.5 collective-permute-start.8
  106.1 3.0 collective-permute-start.7
  109.1 3.4 collective-permute-start.6
  112.5 160.9 %collective-permute-done.3 = bf16[4,128,128]{2,1,0:T(8,128)(2,1)} collective-permute-done((bf16[4,128,128]{2,1,0:T(8,128)(2,1)S(1)}, bf16[4,128,128]{2,1,0:T(8,128)(2,1)}, u32[]{:S(2)}, u32[]{:S(2)}) %collective-permute-start.3) | collective-permute-done | bytes 131104 | tf_op jit(solution)/shard_map/ppermute | solution.py:72
  273.4 0.6 collective-permute-start.4
  274.0 0.9 bitcast_dynamic-update-slice_fusion.6
  274.9 15.7 %collective-permute-done.4 = bf16[4,128,128]{2,1,0:T(8,128)(2,1)S(1)} collective-permute-done((bf16[4,128,128]{2,1,0:T(8,128)(2,1)S(1)}, bf16[4,128,128]{2,1,0:T(8,128)(2,1)S(1)}, u32[]{:S(2)}, u32[]{:S(2)}) %collective-permute-start.4) | collective-permute-done | bytes 131104 | tf_op jit(solution)/shard_map/ppermute | solution.py:72
  290.6 1.3 collective-permute-start.5
  291.9 7.9 %collective-permute-done.5 = bf16[4,128,128]{2,1,0:T(8,128)(2,1)S(1)} collective-permute-done((bf16[4,128,128]{2,1,0:T(8,128)(2,1)S(1)}, bf16[4,128,128]{2,1,0:T(8,128)(2,1)S(1)}, u32[]{:S(2)}, u32[]{:S(2)}) %collective-permute-start.5) | collective-permute-done | bytes 131104 | tf_op jit(solution)/shard_map/ppermute | solution.py:72
  300.0 0.8 gather_fusion.2
  300.7 3.5 fusion.12
  304.2 10.2 %convolution_convert_fusion = bf16[512,1024]{1,0:T(8,128)(2,1)} fusion(bf16[4096,512]{1,0:T(8,128)(2,1)} %bitcast.76, bf16[4096,1024]{1,0:T(8,128)(2,1)} %all-gather.2.cloned.1.call-done), kind=kOutput, calls=%fused_computation.22 | convolution fusion | flops 4295491584 | bytes 13631488 | tf_op jit(solution)/shard_map/dot_general | solution.py:79
  314.4 5.7 %fusion.45 = f32[4096,128]{1,0:T(8,128)S(1)} fusion(bf16[4096,1024]{1,0:T(8,128)(2,1)} %bitcast.33, bf16[128,1024]{1,0:T(8,128)(2,1)S(1)} %copy-done.3), kind=kOutput, calls=%fused_computation.110 | convolution fusion | flops 1073741824 | bytes 10747904 | tf_op jit(solution)/shard_map/dot_general | solution.py:48
  320.1 2.0 copy.52
  322.1 8.5 %select_reduce_fusion = bf16[128,128]{1,0:T(8,128)(2,1)S(1)} fusion(f32[128,32,128]{2,1,0:T(8,128)} %copy.52, s32[128,128]{1,0:T(8,128)S(1)} %copy-done.5, s32[128,128]{1,0:T(8,128)S(1)} %get-tuple-element.15), kind=kOutput, calls=%fused_computation.19 | convolution fusion | flops 808960000 | bytes 2260992 | tf_op jit(solution)/shard_map/tpc,toc->tpo/dot_general | solution.py:52
  330.6 0.1 copy.53
  330.7 17.3 %psum.7 = bf16[128,4,32]{0,2,1:T(8,128)(2,1)S(1)} all-reduce(bf16[128,4,32]{0,2,1:T(8,128)(2,1)S(1)} %bitcast.81), channel_id=1, replica_groups=mesh['mem'=32,'pipe'=4,'dp'=2] {'pipe'}, use_global_device_ids=true, to_apply=%region_3.4 | all-reduce | flops 16384 | bytes 65536 | tf_op jit(solution)/shard_map/psum | solution.py:56
  348.0 0.7 fusion.22
  348.7 5.6 %fusion.17 = bf16[128,1024]{1,0:T(8,128)(2,1)} fusion(bf16[32,128,1024]{2,1,0:T(8,128)(2,1)} %all-to-all-done.1, bf16[128,32,128]{2,1,0:T(8,128)(2,1)S(1)} %copy-done.2), kind=kOutput, calls=%fused_computation.25 | convolution fusion | flops 1073872896 | bytes 9699328 | tf_op jit(solution)/shard_map/dot_general | solution.py:45
  (34 shorter events, 0.3 us)
Async XLA Ops:
  7.2 19.6 %copy-start = (bf16[512,1024]{1,0:T(8,128)(2,1)S(1)}, bf16[512,1024]{1,0:T(8,128)(2,1)}, u32[]{:S(2)}) copy-start(bf16[512,1024]{1,0:T(8,128)(2,1)} %param.5) | copy-start | bytes 3145732
  7.2 19.6 %all-to-all-start = ((s32[32,1,128]{2,1,0:T(1,128)}), s32[32,1,128]{2,1,0:T(1,128)S(1)}, u32[]{:S(2)}, u32[]{:S(2)}) async-start(s32[32,1,128]{2,1,0:T(1,128)} %bitcast.85), calls=%async_computation | async-start | bytes 32768 | tf_op jit(solution)/shard_map/all_to_all | solution.py:34
  18.9 285.3 %all-gather.2.cloned.1.call-start = ((), (), s32[]{:S(2)}) async-start(), calls=%async_computation.2 | async-start | bytes 8650752 | tf_op jit(solution)/shard_map/all_gather | solution.py:15
  33.5 7.8 %copy-start.6 = (s32[128,4,32]{0,2,1:T(8,128)S(1)}, s32[128,4,32]{0,2,1:T(8,128)}, u32[]{:S(2)}) copy-start(s32[128,4,32]{0,2,1:T(8,128)} %param.9) | copy-start | bytes 196612
  33.5 280.8 %all-to-all-start.1 = ((bf16[32,128,1024]{2,1,0:T(8,128)(2,1)}), bf16[32,128,1024]{2,1,0:T(8,128)(2,1)}, u32[]{:S(2)}, u32[]{:S(2)}) async-start(bf16[32,128,1024]{2,1,0:T(8,128)(2,1)} %bitcast.74), calls=%async_computation.1 | async-start | bytes 16777216 | tf_op jit(solution)/shard_map/all_to_all | solution.py:40
  41.5 7.4 %copy-start.4 = (s32[128,128]{1,0:T(8,128)}, s32[128,128]{1,0:T(8,128)S(1)}, u32[]{:S(2)}) copy-start(s32[128,128]{1,0:T(8,128)S(1)} %get-tuple-element.16) | copy-start | bytes 196612
  47.4 1.1 copy-start.1
  49.9 34.5 %collective-permute-start.2 = (bf16[8,128,128]{2,1,0:T(8,128)(2,1)S(1)}, bf16[8,128,128]{2,1,0:T(8,128)(2,1)S(1)}, u32[]{:S(2)}, u32[]{:S(2)}) collective-permute-start(bf16[8,128,128]{2,1,0:T(8,128)(2,1)S(1)} %get-tuple-element.12), channel_id=1, source_target_pairs={{0,24},{8,0},{16,8},{24,16},{32,56},{40,32},{48,40},{56,48},{64,88... | collective-permute-start | bytes 786440 | tf_op jit(solution)/shard_map/ppermute | solution.py:67
  50.9 46.8 %collective-permute-start.1 = (bf16[8,128,128]{2,1,0:T(8,128)(2,1)S(1)}, bf16[8,128,128]{2,1,0:T(8,128)(2,1)S(1)}, u32[]{:S(2)}, u32[]{:S(2)}) collective-permute-start(bf16[8,128,128]{2,1,0:T(8,128)(2,1)S(1)} %get-tuple-element.13), channel_id=1, source_target_pairs={{0,16},{8,24},{16,0},{24,8},{32,48},{40,56},{48,32},{56,40},{64,80... | collective-permute-start | bytes 786440 | tf_op jit(solution)/shard_map/ppermute | solution.py:67
  51.9 45.7 %collective-permute-start = (bf16[8,128,128]{2,1,0:T(8,128)(2,1)S(1)}, bf16[8,128,128]{2,1,0:T(8,128)(2,1)S(1)}, u32[]{:S(2)}, u32[]{:S(2)}) collective-permute-start(bf16[8,128,128]{2,1,0:T(8,128)(2,1)S(1)} %get-tuple-element.14), channel_id=1, source_target_pairs={{0,8},{8,16},{16,24},{24,0},{32,40},{40,48},{48,56},{56,32},{64,72... | collective-permute-start | bytes 786440 | tf_op jit(solution)/shard_map/ppermute | solution.py:67
  98.9 174.5 %collective-permute-start.3 = (bf16[4,128,128]{2,1,0:T(8,128)(2,1)S(1)}, bf16[4,128,128]{2,1,0:T(8,128)(2,1)}, u32[]{:S(2)}, u32[]{:S(2)}) collective-permute-start(bf16[4,128,128]{2,1,0:T(8,128)(2,1)S(1)} %get-tuple-element.9), channel_id=1, source_target_pairs={{0,32},{8,40},{16,48},{24,56},{32,64},{40,72},{48,80},{56,88},{64,... | collective-permute-start | bytes 393224 | tf_op jit(solution)/shard_map/ppermute | solution.py:72
  99.2 200.8 %collective-permute-start.9 = (bf16[4,128,128]{2,1,0:T(8,128)(2,1)S(1)}, bf16[4,128,128]{2,1,0:T(8,128)(2,1)S(1)}, u32[]{:S(2)}, u32[]{:S(2)}) collective-permute-start(bf16[4,128,128]{2,1,0:T(8,128)(2,1)S(1)} %get-tuple-element.3), channel_id=1, source_target_pairs={{0,224},{8,232},{16,240},{24,248},{32,0},{40,8},{48,16},{56,24},{6... | collective-permute-start | bytes 393224 | tf_op jit(solution)/shard_map/ppermute | solution.py:72
  104.6 195.3 %collective-permute-start.8 = (bf16[4,128,128]{2,1,0:T(8,128)(2,1)S(1)}, bf16[4,128,128]{2,1,0:T(8,128)(2,1)S(1)}, u32[]{:S(2)}, u32[]{:S(2)}) collective-permute-start(bf16[4,128,128]{2,1,0:T(8,128)(2,1)S(1)} %get-tuple-element.4), channel_id=1, source_target_pairs={{0,192},{8,200},{16,208},{24,216},{32,224},{40,232},{48,240},{56,2... | collective-permute-start | bytes 393224 | tf_op jit(solution)/shard_map/ppermute | solution.py:72
  106.1 193.8 %collective-permute-start.7 = (bf16[4,128,128]{2,1,0:T(8,128)(2,1)S(1)}, bf16[4,128,128]{2,1,0:T(8,128)(2,1)S(1)}, u32[]{:S(2)}, u32[]{:S(2)}) collective-permute-start(bf16[4,128,128]{2,1,0:T(8,128)(2,1)S(1)} %get-tuple-element.5), channel_id=1, source_target_pairs={{0,160},{8,168},{16,176},{24,184},{32,192},{40,200},{48,208},{56,2... | collective-permute-start | bytes 393224 | tf_op jit(solution)/shard_map/ppermute | solution.py:72
  109.1 190.7 %collective-permute-start.6 = (bf16[4,128,128]{2,1,0:T(8,128)(2,1)S(1)}, bf16[4,128,128]{2,1,0:T(8,128)(2,1)S(1)}, u32[]{:S(2)}, u32[]{:S(2)}) collective-permute-start(bf16[4,128,128]{2,1,0:T(8,128)(2,1)S(1)} %get-tuple-element.6), channel_id=1, source_target_pairs={{0,128},{8,136},{16,144},{24,152},{32,160},{40,168},{48,176},{56,1... | collective-permute-start | bytes 393224 | tf_op jit(solution)/shard_map/ppermute | solution.py:72
  273.4 17.2 %collective-permute-start.4 = (bf16[4,128,128]{2,1,0:T(8,128)(2,1)S(1)}, bf16[4,128,128]{2,1,0:T(8,128)(2,1)S(1)}, u32[]{:S(2)}, u32[]{:S(2)}) collective-permute-start(bf16[4,128,128]{2,1,0:T(8,128)(2,1)S(1)} %get-tuple-element.8), channel_id=1, source_target_pairs={{0,64},{8,72},{16,80},{24,88},{32,96},{40,104},{48,112},{56,120},{... | collective-permute-start | bytes 393224 | tf_op jit(solution)/shard_map/ppermute | solution.py:72
  290.6 9.2 %collective-permute-start.5 = (bf16[4,128,128]{2,1,0:T(8,128)(2,1)S(1)}, bf16[4,128,128]{2,1,0:T(8,128)(2,1)S(1)}, u32[]{:S(2)}, u32[]{:S(2)}) collective-permute-start(bf16[4,128,128]{2,1,0:T(8,128)(2,1)S(1)} %get-tuple-element.7), channel_id=1, source_target_pairs={{0,96},{8,104},{16,112},{24,120},{32,128},{40,136},{48,144},{56,15... | collective-permute-start | bytes 393224 | tf_op jit(solution)/shard_map/ppermute | solution.py:72
  304.2 10.2 %copy-start.3 = (bf16[128,1024]{1,0:T(8,128)(2,1)S(1)}, bf16[128,1024]{1,0:T(8,128)(2,1)}, u32[]{:S(2)}) copy-start(bf16[128,1024]{1,0:T(8,128)(2,1)} %param.6) | copy-start | bytes 786436
  320.1 2.0 copy-start.5
  322.1 26.6 %copy-start.2 = (bf16[128,32,128]{2,1,0:T(8,128)(2,1)S(1)}, bf16[128,32,128]{2,1,0:T(8,128)(2,1)}, u32[]{:S(2)}) copy-start(bf16[128,32,128]{2,1,0:T(8,128)(2,1)} %copy-done.1) | copy-start | bytes 3145732
Sparse Core Ops, SparseCore 0:
  22.3 220.4 all-gather.1

commit v2 on v0

--- a/solution.py
+++ b/solution.py
@@ -31,8 +31,14 @@
         precision=highest,
         preferred_element_type=jnp.float32,
     ).astype(jnp.bfloat16)
-    asked = lax.all_to_all(row_lists[0], "mem", split_axis=0, concat_axis=0, tiled=True)
-    asked = asked.reshape(owners, cap_slots)
+    digit = 32
+    shifted = row_lists[0] + 1
+    digits = jnp.stack([shifted // digit, shifted % digit], axis=1).astype(jnp.bfloat16)
+    outgoing = jnp.concatenate([jnp.swapaxes(combined, 0, 1), digits], axis=1)
+    incoming = lax.all_to_all(outgoing, "mem", 0, 0, tiled=True)
+    comb_in = incoming[:, :tokens_here]
+    got_digits = incoming[:, tokens_here:].astype(jnp.int32)
+    asked = got_digits[:, 0] * digit + got_digits[:, 1] - 1
     row_hot = (asked[..., None] == jnp.arange(table_rows, dtype=jnp.int32)).astype(jnp.bfloat16)
     looked = jnp.dot(
         row_hot.reshape(slot_count, table_rows), values, preferred_element_type=jnp.float32
@@ -55,8 +61,6 @@
     partial_dots = jnp.sum(picked * owner_hot, axis=-1).reshape(weights.shape)
     full_dots = lax.psum(partial_dots.astype(jnp.bfloat16), "pipe").astype(jnp.float32)
     grad_scores = weights * (full_dots - jnp.sum(weights * full_dots, axis=-1, keepdims=True))
-    comb_in = lax.all_to_all(jnp.swapaxes(combined, 0, 1), "mem", 0, 0, tiled=True)
-    comb_in = comb_in.reshape(owners, tokens_here, cap_slots)
     in_rows = jnp.einsum("stc,scr->str", comb_in, row_hot, preferred_element_type=jnp.float32)
     in_rows = in_rows.astype(jnp.bfloat16)
     grad_full = lax.dot_general(

time: 349 us -> 348 us (level)
  starting transfers between devices: 26.7 us -> 17.6 us
  waiting for transfers between devices: 233 us -> 242 us
    all_to_all x1, waiting for transfers between devices: 46.1 us -> 60.2 us  [body(): lax.all_to_all(looked.reshape(owners, cap_slots, width), 'mem', 0, 0, til...]
    all_gather x1, waiting for transfers between devices: 164 us -> 150 us  [body(): all_cot = lax.all_gather(cotangent, 'mem', axis=0, tiled=True)]
    all_to_all x2 -> x1, starting transfers between devices: 21.5 us -> 11.6 us  [body(): incoming = lax.all_to_all(outgoing, 'mem', 0, 0, tiled=True)]
    all_to_all x2 -> x1, waiting for transfers between devices: 22.5 us -> 31 us  [body(): incoming = lax.all_to_all(outgoing, 'mem', 0, 0, tiled=True)]
  transfers between devices with their start and end apart: 4 -> 3, of which waited for: 3 -> 3; matrix products, arithmetic and copies ran while one was open for 9% -> 6% of each run, Pallas kernels for 0% -> 0%
where the time goes in v2:
time: 348 us; the launch traced here: 346 us
  waiting for transfers between devices  242 us (70%)
  matrix products  46 us (13%)
  starting transfers between devices  17.6 us (5%)
  blocking collectives  17.6 us (5%)
  between operations  14.2 us (4%)
  local copies, waits for them, and re-layouts  5.63 us (2%)
    all_gather x1, waiting for transfers between devices, body(): all_cot = lax.all_gather(cotangent, 'mem', axis=0, tiled=True)  150 us
    all_to_all x1, waiting for transfers between devices, body(): lax.all_to_all(looked.reshape(owners, cap_slots, width), 'mem', 0, 0, til...  60.2 us
    all_to_all x1, waiting for transfers between devices, body(): incoming = lax.all_to_all(outgoing, 'mem', 0, 0, tiled=True)  31 us
    psum x1, blocking collectives, body(): lax.psum(partial_dots.astype(jnp.bfloat16), 'pipe').astype(jnp.float32)  17.6 us
    all_to_all x1, starting transfers between devices, body(): incoming = lax.all_to_all(outgoing, 'mem', 0, 0, tiled=True)  11.6 us
    dot_general x1, matrix products, body(): lax.dot_general(in_rows.reshape(slot_count, table_rows), all_cot, (((0,),...  10.2 us
    dot_general x1, matrix products, body(): jnp.einsum('tpc,toc->tpo', place_hot, products, precision=highest, prefer...  8.49 us
  transfers between devices with their start and end apart: 3, of which 3 were waited for; matrix products, arithmetic and copies ran while one was open for 6% of the time, Pallas kernels for 0%

profile of v2, /device:TPU:6, one launch (start us, length us, event | category | flops | bytes accessed | tf_op | source)
XLA Modules:
  0.0 345.8 jit_solution(3037377897166639019)
XLA Ops:
  7.2 0.0 copy-start
  7.2 0.8 fusion.31
  8.0 1.0 fusion.19
  9.0 0.1 copy.30
  9.1 0.9 copy.26
  10.0 0.1 add_select_fusion.1
  10.1 0.0 copy-start.4
  10.1 5.9 %fusion.14 = bf16[128,32,128]{2,1,0:T(8,128)(2,1)S(1)} fusion(s32[128,128]{1,0:T(8,128)S(1)} %get-tuple-element.4, f32[128,128]{1,0:T(8,128)S(1)} %copy.30, s32[128,128]{1,0:T(8,128)S(1)} %get-tuple-element.3), kind=kOutput, calls=%fused_computation.20 | convolution fusion | flops 808976384 | bytes 1245184 | tf_op jit(solution)/shard_map/tpo,tpc->toc/dot_general | solution.py:27
  16.0 0.0 copy-done.4
  16.0 0.0 copy-start.1
  16.0 1.0 copy-done.1
  17.0 0.1 pad_maximum_fusion
  17.2 1.4 copy.31
  18.6 11.6 %all-to-all-start = ((bf16[32,130,128]{2,1,0:T(8,128)(2,1)}), bf16[32,130,128]{2,1,0:T(8,128)(2,1)S(1)}, u32[]{:S(2)}, u32[]{:S(2)}) async-start(bf16[32,130,128]{2,1,0:T(8,128)(2,1)} %copy.31), calls=%async_computation | async-start | bytes 2228224 | tf_op jit(solution)/shard_map/all_to_all | solution.py:38
  30.1 0.0 all-gather.2.cloned.1.call-start
  30.2 0.7 all-gather.2.cloned.1.call-update
  30.9 31.0 %all-to-all-done = bf16[32,130,128]{2,1,0:T(8,128)(2,1)S(1)} async-done(((bf16[32,130,128]{2,1,0:T(8,128)(2,1)}), bf16[32,130,128]{2,1,0:T(8,128)(2,1)S(1)}, u32[]{:S(2)}, u32[]{:S(2)}) %all-to-all-start) | async-done | bytes 1064992 | tf_op jit(solution)/shard_map/all_to_all | solution.py:38
  61.9 0.0 copy-done
  61.9 6.8 %fusion.7 = bf16[4096,1024]{1,0:T(8,128)(2,1)} fusion(bf16[512,1024]{1,0:T(8,128)(2,1)S(1)} %copy-done, s32[4096]{0:T(1024)S(1)} %get-tuple-element.6), kind=kOutput, calls=%fused_computation.10 | convolution fusion | flops 4301258752 | bytes 9453568 | tf_op jit(solution)/shard_map/dot_general | solution.py:43
  68.7 6.0 %all-to-all-start.1 = ((bf16[32,128,1024]{2,1,0:T(8,128)(2,1)}), bf16[32,128,1024]{2,1,0:T(8,128)(2,1)}, u32[]{:S(2)}, u32[]{:S(2)}) async-start(bf16[32,128,1024]{2,1,0:T(8,128)(2,1)} %bitcast.53), calls=%async_computation.1 | async-start | bytes 16777216 | tf_op jit(solution)/shard_map/all_to_all | solution.py:46
  74.7 3.4 fusion.12
  78.2 150.2 %all-gather.2.cloned.1.call-done = bf16[4096,1024]{1,0:T(8,128)(2,1)} async-done(((bf16[128,1024]{1,0:T(8,128)(2,1)}), bf16[4096,1024]{1,0:T(8,128)(2,1)}) %all-gather.2.cloned.1.call-update) | async-done | bytes 8388624 | tf_op jit(solution)/shard_map/all_gather | solution.py:15
  228.3 0.0 copy-start.3
  228.3 10.2 %convolution_convert_fusion = bf16[512,1024]{1,0:T(8,128)(2,1)} fusion(bf16[4096,512]{1,0:T(8,128)(2,1)} %bitcast.55, bf16[4096,1024]{1,0:T(8,128)(2,1)} %all-gather.2.cloned.1.call-done), kind=kOutput, calls=%fused_computation.19 | convolution fusion | flops 4295491584 | bytes 13631488 | tf_op jit(solution)/shard_map/dot_general | solution.py:66
  238.5 60.2 %all-to-all-done.1 = bf16[32,128,1024]{2,1,0:T(8,128)(2,1)} async-done(((bf16[32,128,1024]{2,1,0:T(8,128)(2,1)}), bf16[32,128,1024]{2,1,0:T(8,128)(2,1)}, u32[]{:S(2)}, u32[]{:S(2)}) %all-to-all-start.1) | async-done | bytes 8388640 | tf_op jit(solution)/shard_map/all_to_all | solution.py:46
  298.7 0.0 copy-done.3
  298.8 5.7 %fusion.41 = f32[4096,128]{1,0:T(8,128)S(1)} fusion(bf16[4096,1024]{1,0:T(8,128)(2,1)} %bitcast.9, bf16[128,1024]{1,0:T(8,128)(2,1)S(1)} %copy-done.3), kind=kOutput, calls=%fused_computation.64 | convolution fusion | flops 1073741824 | bytes 10747904 | tf_op jit(solution)/shard_map/dot_general | solution.py:54
  304.5 0.0 copy-start.5
  304.5 2.0 copy.34
  306.5 0.0 copy-done.5
  306.5 0.0 copy-start.2
  306.5 8.5 %select_reduce_fusion = bf16[128,128]{1,0:T(8,128)(2,1)S(1)} fusion(f32[128,32,128]{2,1,0:T(8,128)} %copy.34, s32[128,128]{1,0:T(8,128)S(1)} %copy-done.5, s32[128,128]{1,0:T(8,128)S(1)} %get-tuple-element.3), kind=kOutput, calls=%fused_computation.16 | convolution fusion | flops 808960000 | bytes 2260992 | tf_op jit(solution)/shard_map/tpc,toc->tpo/dot_general | solution.py:58
  315.0 0.1 copy.35
  315.1 17.6 %psum.7 = bf16[128,4,32]{0,2,1:T(8,128)(2,1)S(1)} all-reduce(bf16[128,4,32]{0,2,1:T(8,128)(2,1)S(1)} %bitcast.57), channel_id=1, replica_groups=mesh['mem'=32,'pipe'=4,'dp'=2] {'pipe'}, use_global_device_ids=true, to_apply=%region_3.4 | all-reduce | flops 16384 | bytes 65536 | tf_op jit(solution)/shard_map/psum | solution.py:62
  332.7 0.7 fusion.22
  333.3 0.0 copy-done.2
  333.3 5.6 %fusion.17 = bf16[128,1024]{1,0:T(8,128)(2,1)} fusion(bf16[32,128,1024]{2,1,0:T(8,128)(2,1)} %all-to-all-done.1, bf16[128,32,128]{2,1,0:T(8,128)(2,1)S(1)} %copy-done.2), kind=kOutput, calls=%fused_computation.22 | convolution fusion | flops 1073872896 | bytes 9699328 | tf_op jit(solution)/shard_map/dot_general | solution.py:51
  (3 shorter events, 0.0 us)
Async XLA Ops:
  7.2 54.7 %copy-start = (bf16[512,1024]{1,0:T(8,128)(2,1)S(1)}, bf16[512,1024]{1,0:T(8,128)(2,1)}, u32[]{:S(2)}) copy-start(bf16[512,1024]{1,0:T(8,128)(2,1)} %param.5) | copy-start | bytes 3145732
  10.1 5.9 %copy-start.4 = (s32[128,128]{1,0:T(8,128)}, s32[128,128]{1,0:T(8,128)S(1)}, u32[]{:S(2)}) copy-start(s32[128,128]{1,0:T(8,128)S(1)} %get-tuple-element.4) | copy-start | bytes 196612
  16.0 1.0 copy-start.1
  18.6 43.3 %all-to-all-start = ((bf16[32,130,128]{2,1,0:T(8,128)(2,1)}), bf16[32,130,128]{2,1,0:T(8,128)(2,1)S(1)}, u32[]{:S(2)}, u32[]{:S(2)}) async-start(bf16[32,130,128]{2,1,0:T(8,128)(2,1)} %copy.31), calls=%async_computation | async-start | bytes 2228224 | tf_op jit(solution)/shard_map/all_to_all | solution.py:38
  30.1 198.2 %all-gather.2.cloned.1.call-start = ((), (), s32[]{:S(2)}) async-start(), calls=%async_computation.2 | async-start | bytes 8650752 | tf_op jit(solution)/shard_map/all_gather | solution.py:15
  68.7 230.1 %all-to-all-start.1 = ((bf16[32,128,1024]{2,1,0:T(8,128)(2,1)}), bf16[32,128,1024]{2,1,0:T(8,128)(2,1)}, u32[]{:S(2)}, u32[]{:S(2)}) async-start(bf16[32,128,1024]{2,1,0:T(8,128)(2,1)} %bitcast.53), calls=%async_computation.1 | async-start | bytes 16777216 | tf_op jit(solution)/shard_map/all_to_all | solution.py:46
  228.3 70.4 %copy-start.3 = (bf16[128,1024]{1,0:T(8,128)(2,1)S(1)}, bf16[128,1024]{1,0:T(8,128)(2,1)}, u32[]{:S(2)}) copy-start(bf16[128,1024]{1,0:T(8,128)(2,1)} %param.6) | copy-start | bytes 786436
  304.5 2.0 copy-start.5
  306.5 26.8 %copy-start.2 = (bf16[128,32,128]{2,1,0:T(8,128)(2,1)S(1)}, bf16[128,32,128]{2,1,0:T(8,128)(2,1)}, u32[]{:S(2)}) copy-start(bf16[128,32,128]{2,1,0:T(8,128)(2,1)} %copy-done.1) | copy-start | bytes 3145732
Sparse Core Ops, SparseCore 0:
  33.5 194.7 all-gather.1

commit v3 on v0

--- a/solution.py
+++ b/solution.py
@@ -4,15 +4,21 @@
 from jax.sharding import PartitionSpec as P
 
 
+MEM = ("mz", "mx")
+
+
 def body(values, cotangent, scores, row_lists, sel_slot):
-    owners = lax.axis_size("mem")
+    owners = lax.axis_size(MEM)
     tokens_here = cotangent.shape[0]
     cap_slots = row_lists.shape[2]
     slot_count = owners * cap_slots
     width = values.shape[1]
     table_rows = values.shape[0]
     highest = lax.Precision.HIGHEST
-    all_cot = lax.all_gather(cotangent, "mem", axis=0, tiled=True)
+    along_z = lax.all_gather(cotangent, "mz", axis=0, tiled=True)
+    all_cot = lax.all_gather(along_z, "mx", axis=0, tiled=True)
+    all_cot = all_cot.reshape(lax.axis_size("mx"), lax.axis_size("mz"), -1, all_cot.shape[-1])
+    all_cot = jnp.swapaxes(all_cot, 0, 1).reshape(-1, all_cot.shape[-1])
     weights = jax.nn.softmax(scores, axis=-1)
     chosen = sel_slot.reshape(tokens_here, -1)
     owner_of = chosen // cap_slots
@@ -31,14 +37,14 @@
         precision=highest,
         preferred_element_type=jnp.float32,
     ).astype(jnp.bfloat16)
-    asked = lax.all_to_all(row_lists[0], "mem", split_axis=0, concat_axis=0, tiled=True)
+    asked = lax.all_to_all(row_lists[0], MEM, split_axis=0, concat_axis=0, tiled=True)
     asked = asked.reshape(owners, cap_slots)
     row_hot = (asked[..., None] == jnp.arange(table_rows, dtype=jnp.int32)).astype(jnp.bfloat16)
     looked = jnp.dot(
         row_hot.reshape(slot_count, table_rows), values, preferred_element_type=jnp.float32
     ).astype(jnp.bfloat16)
     replied = lax.all_to_all(
-        looked.reshape(owners, cap_slots, width), "mem", 0, 0, tiled=True
+        looked.reshape(owners, cap_slots, width), MEM, 0, 0, tiled=True
     )
     gathered_rows = replied.reshape(slot_count, width)
     flat_comb = combined.reshape(tokens_here, slot_count)
@@ -55,7 +61,7 @@
     partial_dots = jnp.sum(picked * owner_hot, axis=-1).reshape(weights.shape)
     full_dots = lax.psum(partial_dots.astype(jnp.bfloat16), "pipe").astype(jnp.float32)
     grad_scores = weights * (full_dots - jnp.sum(weights * full_dots, axis=-1, keepdims=True))
-    comb_in = lax.all_to_all(jnp.swapaxes(combined, 0, 1), "mem", 0, 0, tiled=True)
+    comb_in = lax.all_to_all(jnp.swapaxes(combined, 0, 1), MEM, 0, 0, tiled=True)
     comb_in = comb_in.reshape(owners, tokens_here, cap_slots)
     in_rows = jnp.einsum("stc,scr->str", comb_in, row_hot, preferred_element_type=jnp.float32)
     in_rows = in_rows.astype(jnp.bfloat16)
@@ -70,21 +76,24 @@
 
 
 def solution(mesh):
+    z_size = 8
+    devices = mesh.devices.reshape((z_size, -1) + mesh.devices.shape[1:])
+    mesh = jax.sharding.Mesh(devices, ("mz", "mx") + mesh.axis_names[1:])
     placed = (
-        P(("dp", "mem"), "pipe"),
-        P(("dp", "mem"), "pipe"),
-        P(("dp", "mem"), None, None),
-        P(("dp", "mem"), None, None),
-        P(("dp", "mem"), None, None),
+        P(("dp",) + MEM, "pipe"),
+        P(("dp",) + MEM, "pipe"),
+        P(("dp",) + MEM, None, None),
+        P(("dp",) + MEM, None, None),
+        P(("dp",) + MEM, None, None),
     )
     return jax.shard_map(
         body,
         mesh=mesh,
         in_specs=placed,
         out_specs=(
-            P(("dp", "mem"), "pipe"),
-            P(("dp", "mem"), "pipe"),
-            P(("dp", "mem"), None, None),
+            P(("dp",) + MEM, "pipe"),
+            P(("dp",) + MEM, "pipe"),
+            P(("dp",) + MEM, None, None),
         ),
         check_vma=False,
     )

time: 349 us -> 323 us (0.926)
  waiting for transfers between devices: 233 us -> 200 us
  local copies, waits for them, and re-layouts: 5.58 us -> 13.9 us
    all_to_all x3, waiting for transfers between devices: 68.6 us -> 24.6 us  [the longest x1 24.6 us: body(): lax.all_to_all(jnp.swapaxes(combined, 0, 1), MEM, 0, 0, tiled=True)]
    all_gather x1 -> x2, waiting for transfers between devices: 164 us -> 174 us  [the longest x1 144 us: body(): all_cot = lax.all_gather(along_z, 'mx', axis=0, tiled=True)]
    transpose x0 -> x1, local copies, waits for them, and re-layouts: none -> 8.33 us  [body(): all_cot = jnp.swapaxes(all_cot, 0, 1).reshape(-1, all_cot.shape[-1])]
  transfers between devices with their start and end apart: 4 -> 5, of which waited for: 3 -> 3; matrix products, arithmetic and copies ran while one was open for 9% -> 11% of each run, Pallas kernels for 0% -> 0%
where the time goes in v3:
time: 323 us; the launch traced here: 320 us
  waiting for transfers between devices  200 us (62%)
  matrix products  44.1 us (14%)
  starting transfers between devices  26.7 us (8%)
  blocking collectives  20 us (6%)
  between operations  14.2 us (4%)
  local copies, waits for them, and re-layouts  13.9 us (4%)
    all_gather x1, waiting for transfers between devices, body(): all_cot = lax.all_gather(along_z, 'mx', axis=0, tiled=True)  144 us
    all_gather x1, waiting for transfers between devices, body(): along_z = lax.all_gather(cotangent, 'mz', axis=0, tiled=True)  30.2 us
    all_to_all x1, waiting for transfers between devices, body(): lax.all_to_all(jnp.swapaxes(combined, 0, 1), MEM, 0, 0, tiled=True)  24.6 us
    psum x1, blocking collectives, body(): lax.psum(partial_dots.astype(jnp.bfloat16), 'pipe').astype(jnp.float32)  20 us
    all_to_all x1, starting transfers between devices, body(): lax.all_to_all(row_lists[0], MEM, split_axis=0, concat_axis=0, tiled=True)  11.7 us
    all_to_all x1, starting transfers between devices, body(): lax.all_to_all(jnp.swapaxes(combined, 0, 1), MEM, 0, 0, tiled=True)  9.78 us
    dot_general x1, matrix products, body(): jnp.einsum('tpc,toc->tpo', place_hot, products, precision=highest, prefer...  8.49 us
    transpose x1, local copies, waits for them, and re-layouts, body(): all_cot = jnp.swapaxes(all_cot, 0, 1).reshape(-1, all_cot.shape[-1])  8.33 us
  transfers between devices with their start and end apart: 5, of which 3 were waited for; matrix products, arithmetic and copies ran while one was open for 11% of the time, Pallas kernels for 0%

profile of v3, /device:TPU:6, one launch (start us, length us, event | category | flops | bytes accessed | tf_op | source)
XLA Modules:
  0.0 320.2 jit_solution(2771327113745670006)
XLA Ops:
  7.2 0.0 copy-start
  7.2 11.7 %all-to-all-start = ((s32[32,1,128]{2,1,0:T(1,128)}), s32[32,1,128]{2,1,0:T(1,128)S(1)}, u32[]{:S(2)}, u32[]{:S(2)}) async-start(s32[32,1,128]{2,1,0:T(1,128)} %bitcast.41), calls=%async_computation | async-start | bytes 32768 | tf_op jit(solution)/shard_map/all_to_all | solution.py:40
  18.9 1.0 fusion.19
  19.8 0.1 copy.47
  19.9 0.9 copy.43
  20.9 0.1 add_select_fusion.1
  21.0 0.0 copy-start.5
  21.0 5.9 %fusion.14 = bf16[128,32,128]{2,1,0:T(8,128)(2,1)S(1)} fusion(s32[128,128]{1,0:T(8,128)S(1)} %get-tuple-element.4, f32[128,128]{1,0:T(8,128)S(1)} %copy.47, s32[128,128]{1,0:T(8,128)S(1)} %get-tuple-element.3), kind=kOutput, calls=%fused_computation.20 | convolution fusion | flops 808976384 | bytes 1245184 | tf_op jit(solution)/shard_map/tpo,tpc->toc/dot_general | solution.py:33
  26.8 0.0 copy-start.1
  26.9 1.0 copy-done.1
  27.8 1.4 copy.49
  29.2 0.0 copy-done.5
  29.2 0.0 all-to-all-done
  29.2 9.8 %all-to-all-start.2 = ((bf16[32,128,128]{2,1,0:T(8,128)(2,1)}), bf16[32,128,128]{2,1,0:T(8,128)(2,1)S(1)}, u32[]{:S(2)}, u32[]{:S(2)}) async-start(bf16[32,128,128]{2,1,0:T(8,128)(2,1)} %copy.49), calls=%async_computation.2 | async-start | bytes 2097152 | tf_op jit(solution)/shard_map/all_to_all | solution.py:64
  39.0 0.0 all-gather.3.cloned.1.call-start
  39.0 0.7 all-gather.3.cloned.1.call-update
  39.7 0.0 copy-done
  39.7 6.8 %fusion.7 = bf16[4096,1024]{1,0:T(8,128)(2,1)} fusion(bf16[512,1024]{1,0:T(8,128)(2,1)S(1)} %copy-done, s32[4096]{0:T(1024)S(1)} %bitcast.38), kind=kOutput, calls=%fused_computation.10 | convolution fusion | flops 4301258752 | bytes 9453568 | tf_op jit(solution)/shard_map/dot_general | solution.py:43
  46.5 24.6 %all-to-all-done.2 = bf16[32,128,128]{2,1,0:T(8,128)(2,1)S(1)} async-done(((bf16[32,128,128]{2,1,0:T(8,128)(2,1)}), bf16[32,128,128]{2,1,0:T(8,128)(2,1)S(1)}, u32[]{:S(2)}, u32[]{:S(2)}) %all-to-all-start.2) | async-done | bytes 1048608 | tf_op jit(solution)/shard_map/all_to_all | solution.py:64
  71.1 5.0 %all-to-all-start.1 = ((bf16[32,128,1024]{2,1,0:T(8,128)(2,1)}), bf16[32,128,1024]{2,1,0:T(8,128)(2,1)}, u32[]{:S(2)}, u32[]{:S(2)}) async-start(bf16[32,128,1024]{2,1,0:T(8,128)(2,1)} %bitcast.31), calls=%async_computation.1 | async-start | bytes 16777216 | tf_op jit(solution)/shard_map/all_to_all | solution.py:46
  76.1 0.2 all-gather.5.cloned.1.call-start
  76.3 30.2 %all-gather.3.cloned.1.call-done = bf16[1024,1024]{1,0:T(8,128)(2,1)} async-done(((bf16[128,1024]{1,0:T(8,128)(2,1)}), bf16[1024,1024]{1,0:T(8,128)(2,1)}) %all-gather.3.cloned.1.call-update) | async-done | bytes 2097168 | tf_op jit(solution)/shard_map/all_gather | solution.py:18
  106.5 0.0 all-gather.5.cloned.1.call-update
  106.6 3.5 %fusion.12 = bf16[32,128,512]{2,1,0:T(8,128)(2,1)} fusion(bf16[32,128,128]{2,1,0:T(8,128)(2,1)S(1)} %all-to-all-done.2, s32[32,128]{1,0:T(8,128)S(1)} %bitcast.39), kind=kOutput, calls=%fused_computation.15 | convolution fusion | flops 541065216 | bytes 5259264 | tf_op jit(solution)/shard_map/stc,scr->str/dot_general | solution.py:66
  110.1 144.1 %all-gather.5.cloned.1.call-done = bf16[4096,1024]{1,0:T(8,128)(2,1)} async-done(((bf16[1024,1024]{1,0:T(8,128)(2,1)}), bf16[4096,1024]{1,0:T(8,128)(2,1)}) %all-gather.5.cloned.1.call-update) | async-done | bytes 8388624 | tf_op jit(solution)/shard_map/all_gather | solution.py:19
  254.2 0.0 copy-start.3
  254.2 8.3 %copy.50 = bf16[8,4,128,1024]{3,2,1,0:T(8,128)(2,1)} copy(bf16[8,4,128,1024]{3,2,0,1:T(8,128)(2,1)} %bitcast.32) | data formatting | bytes 16777216 | tf_op jit(solution)/shard_map/transpose | solution.py:21
  262.6 0.0 copy-done.3
  262.6 0.0 copy-start.4
  262.6 8.1 %convolution_convert_fusion = bf16[512,1024]{1,0:T(8,128)(2,1)} fusion(bf16[4096,512]{1,0:T(8,128)(2,1)S(1)} %bitcast.35, bf16[4096,1024]{1,0:T(8,128)(2,1)} %bitcast.33), kind=kOutput, calls=%fused_computation.19 | convolution fusion | flops 4295491584 | bytes 13631488 | tf_op jit(solution)/shard_map/dot_general | solution.py:68
  270.7 0.0 all-to-all-done.1
  270.7 0.0 copy-done.4
  270.7 5.7 %fusion.32 = f32[4096,128]{1,0:T(8,128)S(1)} fusion(bf16[4096,1024]{1,0:T(8,128)(2,1)} %bitcast.12, bf16[128,1024]{1,0:T(8,128)(2,1)S(1)} %copy-done.4), kind=kOutput, calls=%fused_computation.44 | convolution fusion | flops 1073741824 | bytes 10747904 | tf_op jit(solution)/shard_map/dot_general | solution.py:54
  276.4 0.0 copy-start.6
  276.4 2.0 copy.51
  278.5 0.0 copy-done.6
  278.5 0.0 copy-start.2
  278.5 8.5 %select_reduce_fusion = bf16[128,128]{1,0:T(8,128)(2,1)S(1)} fusion(f32[128,32,128]{2,1,0:T(8,128)} %copy.51, s32[128,128]{1,0:T(8,128)S(1)} %copy-done.6, s32[128,128]{1,0:T(8,128)S(1)} %get-tuple-element.3), kind=kOutput, calls=%fused_computation.16 | convolution fusion | flops 808960000 | bytes 2260992 | tf_op jit(solution)/shard_map/tpc,toc->tpo/dot_general | solution.py:58
  287.0 0.1 copy.52
  287.1 20.0 %psum.7 = bf16[128,4,32]{0,2,1:T(8,128)(2,1)S(1)} all-reduce(bf16[128,4,32]{0,2,1:T(8,128)(2,1)S(1)} %bitcast.37), channel_id=1, replica_groups=mesh['mz'=8,'mx'=4,'pipe'=4,'dp'=2] {'pipe'}, use_global_device_ids=true, to_apply=%region_3.4 | all-reduce | flops 16384 | bytes 65536 | tf_op jit(solution)/shard_map/psum | solution.py:62
  307.1 0.7 fusion.22
  307.7 0.0 copy-done.2
  307.7 5.6 %fusion.17 = bf16[128,1024]{1,0:T(8,128)(2,1)} fusion(bf16[32,128,1024]{2,1,0:T(8,128)(2,1)} %all-to-all-done.1, bf16[128,32,128]{2,1,0:T(8,128)(2,1)S(1)} %copy-done.2), kind=kOutput, calls=%fused_computation.22 | convolution fusion | flops 1073872896 | bytes 9699328 | tf_op jit(solution)/shard_map/dot_general | solution.py:51
Async XLA Ops:
  7.2 32.6 %copy-start = (bf16[512,1024]{1,0:T(8,128)(2,1)S(1)}, bf16[512,1024]{1,0:T(8,128)(2,1)}, u32[]{:S(2)}) copy-start(bf16[512,1024]{1,0:T(8,128)(2,1)} %param.5) | copy-start | bytes 3145732
  7.2 22.0 %all-to-all-start = ((s32[32,1,128]{2,1,0:T(1,128)}), s32[32,1,128]{2,1,0:T(1,128)S(1)}, u32[]{:S(2)}, u32[]{:S(2)}) async-start(s32[32,1,128]{2,1,0:T(1,128)} %bitcast.41), calls=%async_computation | async-start | bytes 32768 | tf_op jit(solution)/shard_map/all_to_all | solution.py:40
  21.0 8.2 %copy-start.5 = (s32[128,128]{1,0:T(8,128)}, s32[128,128]{1,0:T(8,128)S(1)}, u32[]{:S(2)}) copy-start(s32[128,128]{1,0:T(8,128)S(1)} %get-tuple-element.4) | copy-start | bytes 196612
  26.8 1.0 copy-start.1
  29.2 41.9 %all-to-all-start.2 = ((bf16[32,128,128]{2,1,0:T(8,128)(2,1)}), bf16[32,128,128]{2,1,0:T(8,128)(2,1)S(1)}, u32[]{:S(2)}, u32[]{:S(2)}) async-start(bf16[32,128,128]{2,1,0:T(8,128)(2,1)} %copy.49), calls=%async_computation.2 | async-start | bytes 2097152 | tf_op jit(solution)/shard_map/all_to_all | solution.py:64
  39.0 67.6 %all-gather.3.cloned.1.call-start = ((), (), s32[]{:S(2)}) async-start(), calls=%async_computation.3 | async-start | bytes 2359296 | tf_op jit(solution)/shard_map/all_gather | solution.py:18
  71.1 199.6 %all-to-all-start.1 = ((bf16[32,128,1024]{2,1,0:T(8,128)(2,1)}), bf16[32,128,1024]{2,1,0:T(8,128)(2,1)}, u32[]{:S(2)}, u32[]{:S(2)}) async-start(bf16[32,128,1024]{2,1,0:T(8,128)(2,1)} %bitcast.31), calls=%async_computation.1 | async-start | bytes 16777216 | tf_op jit(solution)/shard_map/all_to_all | solution.py:46
  76.1 178.2 %all-gather.5.cloned.1.call-start = ((), (), s32[]{:S(2)}) async-start(), calls=%async_computation.4 | async-start | bytes 10485760 | tf_op jit(solution)/shard_map/all_gather | solution.py:19
  254.2 8.3 %copy-start.3 = (bf16[32,128,512]{2,1,0:T(8,128)(2,1)S(1)}, bf16[32,128,512]{2,1,0:T(8,128)(2,1)}, u32[]{:S(2)}) copy-start(bf16[32,128,512]{2,1,0:T(8,128)(2,1)} %fusion.12) | copy-start | bytes 12582916
  262.6 8.1 %copy-start.4 = (bf16[128,1024]{1,0:T(8,128)(2,1)S(1)}, bf16[128,1024]{1,0:T(8,128)(2,1)}, u32[]{:S(2)}) copy-start(bf16[128,1024]{1,0:T(8,128)(2,1)} %param.6) | copy-start | bytes 786436
  276.4 2.0 copy-start.6
  278.5 29.3 %copy-start.2 = (bf16[128,32,128]{2,1,0:T(8,128)(2,1)S(1)}, bf16[128,32,128]{2,1,0:T(8,128)(2,1)}, u32[]{:S(2)}) copy-start(bf16[128,32,128]{2,1,0:T(8,128)(2,1)} %copy-done.1) | copy-start | bytes 3145732
Sparse Core Ops, SparseCore 0:
  41.6 64.9 all-gather.2
  108.3 145.8 all-gather.4

commit v4 on v3

--- a/solution.py
+++ b/solution.py
@@ -17,8 +17,8 @@
     highest = lax.Precision.HIGHEST
     along_z = lax.all_gather(cotangent, "mz", axis=0, tiled=True)
     all_cot = lax.all_gather(along_z, "mx", axis=0, tiled=True)
-    all_cot = all_cot.reshape(lax.axis_size("mx"), lax.axis_size("mz"), -1, all_cot.shape[-1])
-    all_cot = jnp.swapaxes(all_cot, 0, 1).reshape(-1, all_cot.shape[-1])
+    x_size, z_size = lax.axis_size("mx"), lax.axis_size("mz")
+    gathered_order = [z * x_size + x for x in range(x_size) for z in range(z_size)]
     weights = jax.nn.softmax(scores, axis=-1)
     chosen = sel_slot.reshape(tokens_here, -1)
     owner_of = chosen // cap_slots
@@ -55,15 +55,20 @@
         cotangent, gathered_rows, (((1,), (1,)), ((), ())), preferred_element_type=jnp.float32
     )
     products = products.reshape(tokens_here, owners, cap_slots)
-    picked = jnp.einsum(
-        "tpc,toc->tpo", place_hot, products, precision=highest, preferred_element_type=jnp.float32
-    )
+    upper = products.astype(jnp.bfloat16)
+    lower = (products - upper.astype(jnp.float32)).astype(jnp.bfloat16)
+    place_bf = place_hot.astype(jnp.bfloat16)
+    picked = jnp.einsum("tpc,toc->tpo", place_bf, upper, preferred_element_type=jnp.float32)
+    picked = picked + jnp.einsum("tpc,toc->tpo", place_bf, lower, preferred_element_type=jnp.float32)
     partial_dots = jnp.sum(picked * owner_hot, axis=-1).reshape(weights.shape)
     full_dots = lax.psum(partial_dots.astype(jnp.bfloat16), "pipe").astype(jnp.float32)
     grad_scores = weights * (full_dots - jnp.sum(weights * full_dots, axis=-1, keepdims=True))
     comb_in = lax.all_to_all(jnp.swapaxes(combined, 0, 1), MEM, 0, 0, tiled=True)
     comb_in = comb_in.reshape(owners, tokens_here, cap_slots)
-    in_rows = jnp.einsum("stc,scr->str", comb_in, row_hot, preferred_element_type=jnp.float32)
+    comb_in = comb_in[jnp.array(gathered_order)]
+    asked_in = asked[jnp.array(gathered_order)]
+    hot_in = (asked_in[..., None] == jnp.arange(table_rows, dtype=jnp.int32)).astype(jnp.bfloat16)
+    in_rows = jnp.einsum("stc,scr->str", comb_in, hot_in, preferred_element_type=jnp.float32)
     in_rows = in_rows.astype(jnp.bfloat16)
     grad_full = lax.dot_general(
         in_rows.reshape(slot_count, table_rows),

time: 323 us -> 325 us (level)
  local copies, waits for them, and re-layouts: 13.9 us -> 6.89 us
  matrix products: 44.1 us -> 48.1 us
    transpose x1 -> x0, local copies, waits for them, and re-layouts: 8.33 us -> none  [body(): all_cot = jnp.swapaxes(all_cot, 0, 1).reshape(-1, all_cot.shape[-1])]
    all_to_all x1, waiting for transfers between devices: 0.01 us -> 5.65 us  [body(): lax.all_to_all(looked.reshape(owners, cap_slots, width), MEM, 0, 0, tiled...]
    dot_general x2 -> x3, matrix products: 12 us -> 14 us  [the longest x1 6.7 us: body(): jnp.einsum('tpc,toc->tpo', place_bf, lower, preferred_element_type=jnp.fl...]
  transfers between devices with their start and end apart: 5 -> 5, of which waited for: 3 -> 4; matrix products, arithmetic and copies ran while one was open for 11% -> 10% of each run, Pallas kernels for 0% -> 0%
where the time goes in v4:
time: 325 us; the launch traced here: 319 us
  waiting for transfers between devices  203 us (62%)
  matrix products  48.1 us (15%)
  starting transfers between devices  26.9 us (8%)
  blocking collectives  18.2 us (6%)
  between operations  14.2 us (4%)
  local copies, waits for them, and re-layouts  6.89 us (2%)
    all_gather x1, waiting for transfers between devices, body(): all_cot = lax.all_gather(along_z, 'mx', axis=0, tiled=True)  142 us
    all_gather x1, waiting for transfers between devices, body(): along_z = lax.all_gather(cotangent, 'mz', axis=0, tiled=True)  30.1 us
    all_to_all x1, waiting for transfers between devices, body(): lax.all_to_all(jnp.swapaxes(combined, 0, 1), MEM, 0, 0, tiled=True)  24.6 us
    psum x1, blocking collectives, body(): lax.psum(partial_dots.astype(jnp.bfloat16), 'pipe').astype(jnp.float32)  18.2 us
    all_to_all x1, starting transfers between devices, body(): lax.all_to_all(row_lists[0], MEM, split_axis=0, concat_axis=0, tiled=True)  11.7 us
    dot_general x1, matrix products, body(): lax.dot_general(in_rows.reshape(slot_count, table_rows), all_cot, (((0,),...  10.2 us
    all_to_all x1, starting transfers between devices, body(): lax.all_to_all(jnp.swapaxes(combined, 0, 1), MEM, 0, 0, tiled=True)  9.78 us
    dot_general x1, matrix products, body(): jnp.dot(row_hot.reshape(slot_count, table_rows), values, preferred_elemen...  6.75 us
  transfers between devices with their start and end apart: 5, of which 4 were waited for; matrix products, arithmetic and copies ran while one was open for 10% of the time, Pallas kernels for 0%

profile of v4, /device:TPU:6, one launch (start us, length us, event | category | flops | bytes accessed | tf_op | source)
XLA Modules:
  0.0 319.1 jit_solution(13021929165034681494)
XLA Ops:
  7.2 0.0 copy-start
  7.2 11.7 %all-to-all-start = ((s32[32,1,128]{2,1,0:T(1,128)}), s32[32,1,128]{2,1,0:T(1,128)S(1)}, u32[]{:S(2)}, u32[]{:S(2)}) async-start(s32[32,1,128]{2,1,0:T(1,128)} %bitcast.34), calls=%async_computation | async-start | bytes 32768 | tf_op jit(solution)/shard_map/all_to_all | solution.py:40
  18.9 1.0 fusion.21
  19.8 0.1 copy.42
  19.9 0.9 copy.38
  20.9 0.1 add_select_fusion.1
  21.0 0.0 copy-start.5
  21.0 5.9 %fusion.16 = bf16[128,32,128]{2,1,0:T(8,128)(2,1)S(1)} fusion(s32[128,128]{1,0:T(8,128)S(1)} %get-tuple-element.4, f32[128,128]{1,0:T(8,128)S(1)} %copy.42, s32[128,128]{1,0:T(8,128)S(1)} %get-tuple-element.3), kind=kOutput, calls=%fused_computation.26 | convolution fusion | flops 808976384 | bytes 1245184 | tf_op jit(solution)/shard_map/tpo,tpc->toc/dot_general | solution.py:33
  26.8 0.0 copy-start.1
  26.9 1.0 copy-done.1
  27.8 1.4 copy.44
  29.2 0.0 copy-done.5
  29.2 0.0 all-to-all-done
  29.2 9.8 %all-to-all-start.2 = ((bf16[32,128,128]{2,1,0:T(8,128)(2,1)}), bf16[32,128,128]{2,1,0:T(8,128)(2,1)S(1)}, u32[]{:S(2)}, u32[]{:S(2)}) async-start(bf16[32,128,128]{2,1,0:T(8,128)(2,1)} %copy.44), calls=%async_computation.2 | async-start | bytes 2097152 | tf_op jit(solution)/shard_map/all_to_all | solution.py:66
  39.0 0.0 all-gather.3.cloned.1.call-start
  39.1 0.7 all-gather.3.cloned.1.call-update
  39.8 0.0 copy-done
  39.8 6.7 %fusion.6 = bf16[4096,1024]{1,0:T(8,128)(2,1)} fusion(bf16[512,1024]{1,0:T(8,128)(2,1)S(1)} %copy-done, s32[4096]{0:T(1024)S(1)} %bitcast.29), kind=kOutput, calls=%fused_computation.12 | convolution fusion | flops 4301258752 | bytes 9453568 | tf_op jit(solution)/shard_map/dot_general | solution.py:43
  46.5 24.6 %all-to-all-done.2 = bf16[32,128,128]{2,1,0:T(8,128)(2,1)S(1)} async-done(((bf16[32,128,128]{2,1,0:T(8,128)(2,1)}), bf16[32,128,128]{2,1,0:T(8,128)(2,1)S(1)}, u32[]{:S(2)}, u32[]{:S(2)}) %all-to-all-start.2) | async-done | bytes 1048608 | tf_op jit(solution)/shard_map/all_to_all | solution.py:66
  71.1 0.0 copy-start.7
  71.1 5.1 %all-to-all-start.1 = ((bf16[32,128,1024]{2,1,0:T(8,128)(2,1)}), bf16[32,128,1024]{2,1,0:T(8,128)(2,1)}, u32[]{:S(2)}, u32[]{:S(2)}) async-start(bf16[32,128,1024]{2,1,0:T(8,128)(2,1)} %bitcast.26), calls=%async_computation.1 | async-start | bytes 16777216 | tf_op jit(solution)/shard_map/all_to_all | solution.py:46
  76.2 0.2 all-gather.5.cloned.1.call-start
  76.5 30.1 %all-gather.3.cloned.1.call-done = bf16[1024,1024]{1,0:T(8,128)(2,1)} async-done(((bf16[128,1024]{1,0:T(8,128)(2,1)}), bf16[1024,1024]{1,0:T(8,128)(2,1)}) %all-gather.3.cloned.1.call-update) | async-done | bytes 2097168 | tf_op jit(solution)/shard_map/all_gather | solution.py:18
  106.5 0.0 all-gather.5.cloned.1.call-update
  106.6 0.0 copy-done.7
  106.6 0.6 gather_fusion.1
  107.2 0.7 gather_fusion
  107.9 3.5 %fusion.14 = bf16[32,128,512]{2,1,0:T(8,128)(2,1)} fusion(bf16[32,128,128]{2,1,0:T(8,128)(2,1)S(1)} %gather_fusion, s32[32,128]{1,0:T(8,128)S(1)} %gather_fusion.1), kind=kOutput, calls=%fused_computation.20 | convolution fusion | flops 541065216 | bytes 5259264 | tf_op jit(solution)/shard_map/stc,scr->str/dot_general | solution.py:71
  111.4 142.2 %all-gather.5.cloned.1.call-done = bf16[4096,1024]{1,0:T(8,128)(2,1)} async-done(((bf16[1024,1024]{1,0:T(8,128)(2,1)}), bf16[4096,1024]{1,0:T(8,128)(2,1)}) %all-gather.5.cloned.1.call-update) | async-done | bytes 8388624 | tf_op jit(solution)/shard_map/all_gather | solution.py:19
  253.5 0.0 copy-start.4
  253.6 10.2 %convolution_convert_fusion = bf16[512,1024]{1,0:T(8,128)(2,1)} fusion(bf16[4096,512]{1,0:T(8,128)(2,1)} %bitcast.28, bf16[4096,1024]{1,0:T(8,128)(2,1)} %all-gather.5.cloned.1.call-done), kind=kOutput, calls=%fused_computation.25 | convolution fusion | flops 4295491584 | bytes 13631488 | tf_op jit(solution)/shard_map/dot_general | solution.py:73
  263.7 5.6 %all-to-all-done.1 = bf16[32,128,1024]{2,1,0:T(8,128)(2,1)} async-done(((bf16[32,128,1024]{2,1,0:T(8,128)(2,1)}), bf16[32,128,1024]{2,1,0:T(8,128)(2,1)}, u32[]{:S(2)}, u32[]{:S(2)}) %all-to-all-start.1) | async-done | bytes 8388640 | tf_op jit(solution)/shard_map/all_to_all | solution.py:46
  269.4 0.0 copy-done.4
  269.4 5.7 %fusion.36 = f32[4096,128]{1,0:T(8,128)S(1)} fusion(bf16[4096,1024]{1,0:T(8,128)(2,1)} %bitcast.9, bf16[128,1024]{1,0:T(8,128)(2,1)S(1)} %copy-done.4), kind=kOutput, calls=%fused_computation.53 | convolution fusion | flops 1073741824 | bytes 10747904 | tf_op jit(solution)/shard_map/dot_general | solution.py:54
  275.1 0.0 copy-start.6
  275.1 2.0 copy.45
  277.1 0.0 copy-done.6
  277.1 0.0 copy-start.3
  277.1 6.7 %fusion.7 = f32[128,128,32]{1,2,0:T(8,128)S(1)} fusion(s32[128,128]{1,0:T(8,128)S(1)} %copy-done.6, f32[128,32,128]{2,1,0:T(8,128)} %copy.45), kind=kOutput, calls=%fused_computation.13 | convolution fusion | flops 142606336 | bytes 4259840 | tf_op jit(solution)/shard_map/tpc,toc->tpo/dot_general | solution.py:62
  283.8 0.0 copy-done.3
  283.8 0.0 copy-start.2
  283.9 3.8 %select_reduce_fusion = bf16[128,128]{1,0:T(8,128)(2,1)S(1)} fusion(f32[128,128,32]{1,2,0:T(8,128)S(1)} %fusion.7, s32[128,128]{1,0:T(8,128)S(1)} %copy-done.6, s32[128,128]{1,0:T(8,128)S(1)} %get-tuple-element.3, f32[128,32,128]{2,1,0:T(8,128)S(1)} %copy-done.3), kind=kOutput, calls=%fused_computation.21 | convolution fusion | flops 143114240 | bytes 4358144 | tf_op jit(solution)/shard_map/tpc,toc->tpo/dot_general | solution.py:61
  287.7 0.1 copy.47
  287.8 18.2 %psum.7 = bf16[128,4,32]{0,2,1:T(8,128)(2,1)S(1)} all-reduce(bf16[128,4,32]{0,2,1:T(8,128)(2,1)S(1)} %bitcast.32), channel_id=1, replica_groups=mesh['mz'=8,'mx'=4,'pipe'=4,'dp'=2] {'pipe'}, use_global_device_ids=true, to_apply=%region_3.4 | all-reduce | flops 16384 | bytes 65536 | tf_op jit(solution)/shard_map/psum | solution.py:64
  306.0 0.7 fusion.24
  306.6 0.0 copy-done.2
  306.6 5.6 %fusion.19 = bf16[128,1024]{1,0:T(8,128)(2,1)} fusion(bf16[32,128,1024]{2,1,0:T(8,128)(2,1)} %all-to-all-done.1, bf16[128,32,128]{2,1,0:T(8,128)(2,1)S(1)} %copy-done.2), kind=kOutput, calls=%fused_computation.28 | convolution fusion | flops 1073872896 | bytes 9699328 | tf_op jit(solution)/shard_map/dot_general | solution.py:51
  (1 shorter events, 0.0 us)
Async XLA Ops:
  7.2 32.6 %copy-start = (bf16[512,1024]{1,0:T(8,128)(2,1)S(1)}, bf16[512,1024]{1,0:T(8,128)(2,1)}, u32[]{:S(2)}) copy-start(bf16[512,1024]{1,0:T(8,128)(2,1)} %param.7) | copy-start | bytes 3145732
  7.2 22.1 %all-to-all-start = ((s32[32,1,128]{2,1,0:T(1,128)}), s32[32,1,128]{2,1,0:T(1,128)S(1)}, u32[]{:S(2)}, u32[]{:S(2)}) async-start(s32[32,1,128]{2,1,0:T(1,128)} %bitcast.34), calls=%async_computation | async-start | bytes 32768 | tf_op jit(solution)/shard_map/all_to_all | solution.py:40
  21.0 8.3 %copy-start.5 = (s32[128,128]{1,0:T(8,128)}, s32[128,128]{1,0:T(8,128)S(1)}, u32[]{:S(2)}) copy-start(s32[128,128]{1,0:T(8,128)S(1)} %get-tuple-element.4) | copy-start | bytes 196612
  26.8 1.0 copy-start.1
  29.2 41.9 %all-to-all-start.2 = ((bf16[32,128,128]{2,1,0:T(8,128)(2,1)}), bf16[32,128,128]{2,1,0:T(8,128)(2,1)S(1)}, u32[]{:S(2)}, u32[]{:S(2)}) async-start(bf16[32,128,128]{2,1,0:T(8,128)(2,1)} %copy.44), calls=%async_computation.2 | async-start | bytes 2097152 | tf_op jit(solution)/shard_map/all_to_all | solution.py:66
  39.0 67.5 %all-gather.3.cloned.1.call-start = ((), (), s32[]{:S(2)}) async-start(), calls=%async_computation.3 | async-start | bytes 2359296 | tf_op jit(solution)/shard_map/all_gather | solution.py:18
  71.1 35.5 %copy-start.7 = (s32[32]{0:T(128)S(1)}, s32[32]{0:T(128)}, u32[]{:S(2)}) copy-start(s32[32]{0:T(128)} %constant.46) | copy-start | bytes 388
  71.1 198.3 %all-to-all-start.1 = ((bf16[32,128,1024]{2,1,0:T(8,128)(2,1)}), bf16[32,128,1024]{2,1,0:T(8,128)(2,1)}, u32[]{:S(2)}, u32[]{:S(2)}) async-start(bf16[32,128,1024]{2,1,0:T(8,128)(2,1)} %bitcast.26), calls=%async_computation.1 | async-start | bytes 16777216 | tf_op jit(solution)/shard_map/all_to_all | solution.py:46
  76.2 177.3 %all-gather.5.cloned.1.call-start = ((), (), s32[]{:S(2)}) async-start(), calls=%async_computation.4 | async-start | bytes 10485760 | tf_op jit(solution)/shard_map/all_gather | solution.py:19
  253.5 15.8 %copy-start.4 = (bf16[128,1024]{1,0:T(8,128)(2,1)S(1)}, bf16[128,1024]{1,0:T(8,128)(2,1)}, u32[]{:S(2)}) copy-start(bf16[128,1024]{1,0:T(8,128)(2,1)} %param.8) | copy-start | bytes 786436
  275.1 2.0 copy-start.6
  277.1 6.7 %copy-start.3 = (f32[128,32,128]{2,1,0:T(8,128)S(1)}, f32[128,32,128]{2,1,0:T(8,128)}, u32[]{:S(2)}) copy-start(f32[128,32,128]{2,1,0:T(8,128)} %copy.45) | copy-start | bytes 6291460
  283.8 22.8 %copy-start.2 = (bf16[128,32,128]{2,1,0:T(8,128)(2,1)S(1)}, bf16[128,32,128]{2,1,0:T(8,128)(2,1)}, u32[]{:S(2)}) copy-start(bf16[128,32,128]{2,1,0:T(8,128)(2,1)} %copy-done.1) | copy-start | bytes 3145732
Sparse Core Ops, SparseCore 0:
  41.6 64.8 all-gather.2
  108.3 145.1 all-gather.4

commit v5 on v4

--- a/solution.py
+++ b/solution.py
@@ -55,13 +55,15 @@
         cotangent, gathered_rows, (((1,), (1,)), ((), ())), preferred_element_type=jnp.float32
     )
     products = products.reshape(tokens_here, owners, cap_slots)
-    upper = products.astype(jnp.bfloat16)
-    lower = (products - upper.astype(jnp.float32)).astype(jnp.bfloat16)
-    place_bf = place_hot.astype(jnp.bfloat16)
-    picked = jnp.einsum("tpc,toc->tpo", place_bf, upper, preferred_element_type=jnp.float32)
-    picked = picked + jnp.einsum("tpc,toc->tpo", place_bf, lower, preferred_element_type=jnp.float32)
+    picked = jnp.einsum(
+        "tpc,toc->tpo", place_hot, products, precision=highest, preferred_element_type=jnp.float32
+    )
     partial_dots = jnp.sum(picked * owner_hot, axis=-1).reshape(weights.shape)
-    full_dots = lax.psum(partial_dots.astype(jnp.bfloat16), "pipe").astype(jnp.float32)
+    flat_dots = partial_dots.reshape(tokens_here, -1)
+    room = jnp.zeros((tokens_here, 3 * flat_dots.shape[1]), jnp.float32)
+    padded = jnp.concatenate([flat_dots, room], axis=1)
+    gathered = lax.all_gather(padded, "pipe", axis=0)[:, :, : flat_dots.shape[1]]
+    full_dots = jnp.sum(gathered, axis=0).reshape(weights.shape)
     grad_scores = weights * (full_dots - jnp.sum(weights * full_dots, axis=-1, keepdims=True))
     comb_in = lax.all_to_all(jnp.swapaxes(combined, 0, 1), MEM, 0, 0, tiled=True)
     comb_in = comb_in.reshape(owners, tokens_here, cap_slots)

time: 325 us -> 335 us (1.031); the launches traced: 319 us -> 334 us
  waiting for transfers between devices: 203 us -> 235 us
  blocking collectives: 18.2 us -> 0 us
    all_gather x1, waiting for transfers between devices: 142 us -> 2.77 us  [body(): all_cot = lax.all_gather(along_z, 'mx', axis=0, tiled=True)]
    all_to_all x1, waiting for transfers between devices: 5.65 us -> 101 us  [body(): lax.all_to_all(looked.reshape(owners, cap_slots, width), MEM, 0, 0, tiled...]
    all_gather x1, waiting for transfers between devices: 30.1 us -> 96.8 us  [body(): along_z = lax.all_gather(cotangent, 'mz', axis=0, tiled=True)]
    psum x1 -> x0, blocking collectives: 18.2 us -> none  [body(): lax.psum(partial_dots.astype(jnp.bfloat16), 'pipe').astype(jnp.float32)]
    all_gather x0 -> x1, waiting for transfers between devices: none -> 13.4 us  [body(): gathered = lax.all_gather(padded, 'pipe', axis=0)[:, :, :flat_dots.shape[1]]]
    all_to_all x1, waiting for transfers between devices: 24.6 us -> 20.7 us  [body(): lax.all_to_all(jnp.swapaxes(combined, 0, 1), MEM, 0, 0, tiled=True)]
    dot_general x2 -> x1, matrix products: 10.5 us -> 8.4 us  [body(): jnp.einsum('tpc,toc->tpo', place_hot, products, precision=highest, prefer...]
  transfers between devices with their start and end apart: 5 -> 6, of which waited for: 4 -> 5; matrix products, arithmetic and copies ran while one was open for 10% -> 16% of each run, Pallas kernels for 0% -> 0%
where the time goes in v5:
time: 335 us; the launch traced here: 334 us
  waiting for transfers between devices  235 us (70%)
  matrix products  46 us (14%)
  starting transfers between devices  27.5 us (8%)
  between operations  13.9 us (4%)
  local copies, waits for them, and re-layouts  8.35 us (2%)
    all_to_all x1, waiting for transfers between devices, body(): lax.all_to_all(looked.reshape(owners, cap_slots, width), MEM, 0, 0, tiled...  101 us
    all_gather x1, waiting for transfers between devices, body(): along_z = lax.all_gather(cotangent, 'mz', axis=0, tiled=True)  96.8 us
    all_to_all x1, waiting for transfers between devices, body(): lax.all_to_all(jnp.swapaxes(combined, 0, 1), MEM, 0, 0, tiled=True)  20.7 us
    all_gather x1, waiting for transfers between devices, body(): gathered = lax.all_gather(padded, 'pipe', axis=0)[:, :, :flat_dots.shape[1]]  13.4 us
    all_to_all x1, starting transfers between devices, body(): lax.all_to_all(row_lists[0], MEM, split_axis=0, concat_axis=0, tiled=True)  11.7 us
    dot_general x1, matrix products, body(): lax.dot_general(in_rows.reshape(slot_count, table_rows), all_cot, (((0,),...  10.2 us
    all_to_all x1, starting transfers between devices, body(): lax.all_to_all(jnp.swapaxes(combined, 0, 1), MEM, 0, 0, tiled=True)  9.78 us
    dot_general x1, matrix products, body(): jnp.einsum('tpc,toc->tpo', place_hot, products, precision=highest, prefer...  8.4 us
  transfers between devices with their start and end apart: 6, of which 5 were waited for; matrix products, arithmetic and copies ran while one was open for 16% of the time, Pallas kernels for 0%

profile of v5, /device:TPU:6, one launch (start us, length us, event | category | flops | bytes accessed | tf_op | source)
XLA Modules:
  0.0 333.9 jit_solution(17259298344901055691)
XLA Ops:
  7.2 0.0 copy-start
  7.2 11.7 %all-to-all-start = ((s32[32,1,128]{2,1,0:T(1,128)}), s32[32,1,128]{2,1,0:T(1,128)S(1)}, u32[]{:S(2)}, u32[]{:S(2)}) async-start(s32[32,1,128]{2,1,0:T(1,128)} %bitcast.38), calls=%async_computation | async-start | bytes 32768 | tf_op jit(solution)/shard_map/all_to_all | solution.py:40
  18.9 1.0 fusion.19
  19.8 0.1 copy.48
  19.9 0.9 copy.44
  20.9 0.1 add_select_fusion.1
  21.0 0.0 copy-start.4
  21.0 5.9 %fusion.14 = bf16[128,32,128]{2,1,0:T(8,128)(2,1)S(1)} fusion(s32[128,128]{1,0:T(8,128)S(1)} %get-tuple-element.4, f32[128,128]{1,0:T(8,128)S(1)} %copy.48, s32[128,128]{1,0:T(8,128)S(1)} %get-tuple-element.3), kind=kOutput, calls=%fused_computation.22 | convolution fusion | flops 808976384 | bytes 1245184 | tf_op jit(solution)/shard_map/tpo,tpc->toc/dot_general | solution.py:33
  26.8 0.0 copy-start.1
  26.9 1.0 copy-done.1
  27.8 1.4 copy.50
  29.2 0.0 copy-done.4
  29.2 0.0 all-to-all-done
  29.2 9.8 %all-to-all-start.2 = ((bf16[32,128,128]{2,1,0:T(8,128)(2,1)}), bf16[32,128,128]{2,1,0:T(8,128)(2,1)S(1)}, u32[]{:S(2)}, u32[]{:S(2)}) async-start(bf16[32,128,128]{2,1,0:T(8,128)(2,1)} %copy.50), calls=%async_computation.2 | async-start | bytes 2097152 | tf_op jit(solution)/shard_map/all_to_all | solution.py:68
  39.0 0.0 copy-done
  39.0 6.8 %fusion.7 = bf16[4096,1024]{1,0:T(8,128)(2,1)} fusion(bf16[512,1024]{1,0:T(8,128)(2,1)S(1)} %copy-done, s32[4096]{0:T(1024)S(1)} %bitcast.32), kind=kOutput, calls=%fused_computation.12 | convolution fusion | flops 4301258752 | bytes 9453568 | tf_op jit(solution)/shard_map/dot_general | solution.py:43
  45.8 20.7 %all-to-all-done.2 = bf16[32,128,128]{2,1,0:T(8,128)(2,1)S(1)} async-done(((bf16[32,128,128]{2,1,0:T(8,128)(2,1)}), bf16[32,128,128]{2,1,0:T(8,128)(2,1)S(1)}, u32[]{:S(2)}, u32[]{:S(2)}) %all-to-all-start.2) | async-done | bytes 1048608 | tf_op jit(solution)/shard_map/all_to_all | solution.py:68
  66.5 5.8 %all-to-all-start.1 = ((bf16[32,128,1024]{2,1,0:T(8,128)(2,1)}), bf16[32,128,1024]{2,1,0:T(8,128)(2,1)}, u32[]{:S(2)}, u32[]{:S(2)}) async-start(bf16[32,128,1024]{2,1,0:T(8,128)(2,1)} %bitcast.29), calls=%async_computation.1 | async-start | bytes 16777216 | tf_op jit(solution)/shard_map/all_to_all | solution.py:46
  72.3 0.0 all-gather.5.cloned.1.call-start
  72.3 0.7 all-gather.5.cloned.1.call-update
  73.0 0.0 all-gather.7.cloned.1.call-start
  73.0 96.8 %all-gather.5.cloned.1.call-done = bf16[1024,1024]{1,0:T(8,128)(2,1)} async-done(((bf16[128,1024]{1,0:T(8,128)(2,1)}), bf16[1024,1024]{1,0:T(8,128)(2,1)}) %all-gather.5.cloned.1.call-update) | async-done | bytes 2097168 | tf_op jit(solution)/shard_map/all_gather | solution.py:18
  169.8 0.0 all-gather.7.cloned.1.call-update
  169.8 0.0 copy-start.3
  169.8 0.2 all-gather.9.cloned.1.call-start
  170.1 0.0 copy-done.7
  170.1 0.0 copy-start.6
  170.1 0.6 copy-done.6
  170.7 0.6 gather_fusion.1
  171.3 0.9 gather_fusion
  172.1 3.5 %fusion.12 = bf16[32,128,512]{2,1,0:T(8,128)(2,1)} fusion(bf16[32,128,128]{2,1,0:T(8,128)(2,1)S(1)} %gather_fusion, s32[32,128]{1,0:T(8,128)S(1)} %gather_fusion.1), kind=kOutput, calls=%fused_computation.17 | convolution fusion | flops 541065216 | bytes 5259264 | tf_op jit(solution)/shard_map/stc,scr->str/dot_general | solution.py:73
  175.6 101.1 %all-to-all-done.1 = bf16[32,128,1024]{2,1,0:T(8,128)(2,1)} async-done(((bf16[32,128,1024]{2,1,0:T(8,128)(2,1)}), bf16[32,128,1024]{2,1,0:T(8,128)(2,1)}, u32[]{:S(2)}, u32[]{:S(2)}) %all-to-all-start.1) | async-done | bytes 8388640 | tf_op jit(solution)/shard_map/all_to_all | solution.py:46
  276.7 0.0 copy-done.3
  276.7 5.7 %fusion.32 = f32[4096,128]{1,0:T(8,128)S(1)} fusion(bf16[4096,1024]{1,0:T(8,128)(2,1)} %bitcast.9, bf16[128,1024]{1,0:T(8,128)(2,1)S(1)} %copy-done.3), kind=kOutput, calls=%fused_computation.48 | convolution fusion | flops 1073741824 | bytes 10747904 | tf_op jit(solution)/shard_map/dot_general | solution.py:54
  282.4 0.0 copy-start.5
  282.4 2.1 copy.51
  284.5 0.0 copy-done.5
  284.5 8.4 %select_reduce_fusion = f32[128,128]{1,0:T(8,128)S(1)} fusion(f32[128,32,128]{2,1,0:T(8,128)} %copy.51, s32[128,128]{1,0:T(8,128)S(1)} %copy-done.5, s32[128,128]{1,0:T(8,128)S(1)} %get-tuple-element.3), kind=kOutput, calls=%fused_computation.18 | convolution fusion | flops 808960000 | bytes 2293760 | tf_op jit(solution)/shard_map/tpc,toc->tpo/dot_general | solution.py:58
  292.9 0.7 concatenate.3
  293.7 0.0 all-gather.9.cloned.1.call-update
  293.7 2.8 all-gather.7.cloned.1.call-done
  296.5 10.2 %convolution_convert_fusion = bf16[512,1024]{1,0:T(8,128)(2,1)} fusion(bf16[4096,512]{1,0:T(8,128)(2,1)} %bitcast.31, bf16[4096,1024]{1,0:T(8,128)(2,1)} %all-gather.7.cloned.1.call-done), kind=kOutput, calls=%fused_computation.21 | convolution fusion | flops 4295491584 | bytes 13631488 | tf_op jit(solution)/shard_map/dot_general | solution.py:75
  306.7 0.0 copy-done.2
  306.7 5.6 %fusion.17 = bf16[128,1024]{1,0:T(8,128)(2,1)} fusion(bf16[32,128,1024]{2,1,0:T(8,128)(2,1)} %all-to-all-done.1, bf16[128,32,128]{2,1,0:T(8,128)(2,1)S(1)} %copy-done.2), kind=kOutput, calls=%fused_computation.24 | convolution fusion | flops 1073872896 | bytes 9699328 | tf_op jit(solution)/shard_map/dot_general | solution.py:51
  312.3 13.4 %all-gather.9.cloned.1.call-done = f32[512,512]{1,0:T(8,128)} async-done(((f32[128,512]{1,0:T(8,128)}), f32[512,512]{1,0:T(8,128)}) %all-gather.9.cloned.1.call-update) | async-done | bytes 1048592 | tf_op jit(solution)/shard_map/all_gather | solution.py:65
  325.7 1.0 slice_reduce_fusion
  326.6 0.1 copy.52
  326.7 0.7 fusion.22
  (3 shorter events, 0.0 us)
Async XLA Ops:
  7.2 31.8 %copy-start = (bf16[512,1024]{1,0:T(8,128)(2,1)S(1)}, bf16[512,1024]{1,0:T(8,128)(2,1)}, u32[]{:S(2)}) copy-start(bf16[512,1024]{1,0:T(8,128)(2,1)} %param.7) | copy-start | bytes 3145732
  7.2 22.0 %all-to-all-start = ((s32[32,1,128]{2,1,0:T(1,128)}), s32[32,1,128]{2,1,0:T(1,128)S(1)}, u32[]{:S(2)}, u32[]{:S(2)}) async-start(s32[32,1,128]{2,1,0:T(1,128)} %bitcast.38), calls=%async_computation | async-start | bytes 32768 | tf_op jit(solution)/shard_map/all_to_all | solution.py:40
  21.0 8.3 %copy-start.4 = (s32[128,128]{1,0:T(8,128)}, s32[128,128]{1,0:T(8,128)S(1)}, u32[]{:S(2)}) copy-start(s32[128,128]{1,0:T(8,128)S(1)} %get-tuple-element.4) | copy-start | bytes 196612
  26.8 1.0 copy-start.1
  29.2 37.3 %all-to-all-start.2 = ((bf16[32,128,128]{2,1,0:T(8,128)(2,1)}), bf16[32,128,128]{2,1,0:T(8,128)(2,1)S(1)}, u32[]{:S(2)}, u32[]{:S(2)}) async-start(bf16[32,128,128]{2,1,0:T(8,128)(2,1)} %copy.50), calls=%async_computation.2 | async-start | bytes 2097152 | tf_op jit(solution)/shard_map/all_to_all | solution.py:68
  66.5 103.6 %copy-start.7 = (s32[32]{0:T(128)S(1)}, s32[32]{0:T(128)}, u32[]{:S(2)}) copy-start(s32[32]{0:T(128)} %constant.49) | copy-start | bytes 388
  66.5 210.2 %all-to-all-start.1 = ((bf16[32,128,1024]{2,1,0:T(8,128)(2,1)}), bf16[32,128,1024]{2,1,0:T(8,128)(2,1)}, u32[]{:S(2)}, u32[]{:S(2)}) async-start(bf16[32,128,1024]{2,1,0:T(8,128)(2,1)} %bitcast.29), calls=%async_computation.1 | async-start | bytes 16777216 | tf_op jit(solution)/shard_map/all_to_all | solution.py:46
  72.3 97.5 %all-gather.5.cloned.1.call-start = ((), (), s32[]{:S(2)}) async-start(), calls=%async_computation.3 | async-start | bytes 2359296 | tf_op jit(solution)/shard_map/all_gather | solution.py:18
  73.0 223.5 %all-gather.7.cloned.1.call-start = ((), (), s32[]{:S(2)}) async-start(), calls=%async_computation.4 | async-start | bytes 10485760 | tf_op jit(solution)/shard_map/all_gather | solution.py:19
  169.8 106.9 %copy-start.3 = (bf16[128,1024]{1,0:T(8,128)(2,1)S(1)}, bf16[128,1024]{1,0:T(8,128)(2,1)}, u32[]{:S(2)}) copy-start(bf16[128,1024]{1,0:T(8,128)(2,1)} %param.8) | copy-start | bytes 786436
  169.8 155.8 %all-gather.9.cloned.1.call-start = ((), (), s32[]{:S(2)}) async-start(), calls=%async_computation.5 | async-start | bytes 1310720 | tf_op jit(solution)/shard_map/all_gather | solution.py:65
  170.1 0.6 copy-start.6
  282.4 2.1 copy-start.5
  296.5 10.2 %copy-start.2 = (bf16[128,32,128]{2,1,0:T(8,128)(2,1)S(1)}, bf16[128,32,128]{2,1,0:T(8,128)(2,1)}, u32[]{:S(2)}) copy-start(bf16[128,32,128]{2,1,0:T(8,128)(2,1)} %copy-done.1) | copy-start | bytes 3145732
Sparse Core Ops, SparseCore 0:
  74.9 94.8 all-gather.4
  171.6 124.8 all-gather.6
  298.3 27.3 all-gather.8

commit v6 on v5

--- a/solution.py
+++ b/solution.py
@@ -70,13 +70,10 @@
     comb_in = comb_in[jnp.array(gathered_order)]
     asked_in = asked[jnp.array(gathered_order)]
     hot_in = (asked_in[..., None] == jnp.arange(table_rows, dtype=jnp.int32)).astype(jnp.bfloat16)
-    in_rows = jnp.einsum("stc,scr->str", comb_in, hot_in, preferred_element_type=jnp.float32)
+    in_rows = jnp.einsum("stc,scr->rst", comb_in, hot_in, preferred_element_type=jnp.float32)
     in_rows = in_rows.astype(jnp.bfloat16)
-    grad_full = lax.dot_general(
-        in_rows.reshape(slot_count, table_rows),
-        all_cot,
-        (((0,), (0,)), ((), ())),
-        preferred_element_type=jnp.float32,
+    grad_full = jnp.dot(
+        in_rows.reshape(table_rows, slot_count), all_cot, preferred_element_type=jnp.float32
     )
     grad_values = grad_full.astype(jnp.bfloat16)
     return (mem_out, grad_values, grad_scores)

time: 335 us -> 335 us (level)
  no operation moved by 1% of the time
where the time goes in v6:
time: 335 us; the launch traced here: 334 us
  waiting for transfers between devices  235 us (70%)
  matrix products  46 us (14%)
  starting transfers between devices  27.5 us (8%)
  between operations  13.9 us (4%)
  local copies, waits for them, and re-layouts  7.89 us (2%)
    all_to_all x1, waiting for transfers between devices, body(): lax.all_to_all(looked.reshape(owners, cap_slots, width), MEM, 0, 0, tiled...  101 us
    all_gather x1, waiting for transfers between devices, body(): along_z = lax.all_gather(cotangent, 'mz', axis=0, tiled=True)  96.8 us
    all_to_all x1, waiting for transfers between devices, body(): lax.all_to_all(jnp.swapaxes(combined, 0, 1), MEM, 0, 0, tiled=True)  20.7 us
    all_gather x1, waiting for transfers between devices, body(): gathered = lax.all_gather(padded, 'pipe', axis=0)[:, :, :flat_dots.shape[1]]  13.4 us
    all_to_all x1, starting transfers between devices, body(): lax.all_to_all(row_lists[0], MEM, split_axis=0, concat_axis=0, tiled=True)  11.7 us
    dot_general x1, matrix products, body(): jnp.dot(in_rows.reshape(table_rows, slot_count), all_cot, preferred_eleme...  10.2 us
    all_to_all x1, starting transfers between devices, body(): lax.all_to_all(jnp.swapaxes(combined, 0, 1), MEM, 0, 0, tiled=True)  9.78 us
    dot_general x1, matrix products, body(): jnp.einsum('tpc,toc->tpo', place_hot, products, precision=highest, prefer...  8.4 us
  transfers between devices with their start and end apart: 6, of which 5 were waited for; matrix products, arithmetic and copies ran while one was open for 16% of the time, Pallas kernels for 0%

profile of v6, /device:TPU:6, one launch (start us, length us, event | category | flops | bytes accessed | tf_op | source)
XLA Modules:
  0.0 333.9 jit_solution(6415447968812679547)
XLA Ops:
  7.2 0.0 copy-start
  7.2 11.7 %all-to-all-start = ((s32[32,1,128]{2,1,0:T(1,128)}), s32[32,1,128]{2,1,0:T(1,128)S(1)}, u32[]{:S(2)}, u32[]{:S(2)}) async-start(s32[32,1,128]{2,1,0:T(1,128)} %bitcast.39), calls=%async_computation | async-start | bytes 32768 | tf_op jit(solution)/shard_map/all_to_all | solution.py:40
  18.9 1.0 fusion.19
  19.8 0.1 copy.48
  19.9 0.9 copy.44
  20.9 0.1 add_select_fusion.1
  21.0 0.0 copy-start.4
  21.0 5.9 %fusion.14 = bf16[128,32,128]{2,1,0:T(8,128)(2,1)S(1)} fusion(s32[128,128]{1,0:T(8,128)S(1)} %get-tuple-element.4, f32[128,128]{1,0:T(8,128)S(1)} %copy.48, s32[128,128]{1,0:T(8,128)S(1)} %get-tuple-element.3), kind=kOutput, calls=%fused_computation.22 | convolution fusion | flops 808976384 | bytes 1245184 | tf_op jit(solution)/shard_map/tpo,tpc->toc/dot_general | solution.py:33
  26.8 0.0 copy-start.1
  26.9 1.0 copy-done.1
  27.8 1.4 copy.50
  29.2 0.0 copy-done.4
  29.2 0.0 all-to-all-done
  29.2 9.8 %all-to-all-start.2 = ((bf16[32,128,128]{2,1,0:T(8,128)(2,1)}), bf16[32,128,128]{2,1,0:T(8,128)(2,1)S(1)}, u32[]{:S(2)}, u32[]{:S(2)}) async-start(bf16[32,128,128]{2,1,0:T(8,128)(2,1)} %copy.50), calls=%async_computation.2 | async-start | bytes 2097152 | tf_op jit(solution)/shard_map/all_to_all | solution.py:68
  39.0 0.0 copy-done
  39.0 6.8 %fusion.7 = bf16[4096,1024]{1,0:T(8,128)(2,1)} fusion(bf16[512,1024]{1,0:T(8,128)(2,1)S(1)} %copy-done, s32[4096]{0:T(1024)S(1)} %bitcast.33), kind=kOutput, calls=%fused_computation.12 | convolution fusion | flops 4301258752 | bytes 9453568 | tf_op jit(solution)/shard_map/dot_general | solution.py:43
  45.8 20.7 %all-to-all-done.2 = bf16[32,128,128]{2,1,0:T(8,128)(2,1)S(1)} async-done(((bf16[32,128,128]{2,1,0:T(8,128)(2,1)}), bf16[32,128,128]{2,1,0:T(8,128)(2,1)S(1)}, u32[]{:S(2)}, u32[]{:S(2)}) %all-to-all-start.2) | async-done | bytes 1048608 | tf_op jit(solution)/shard_map/all_to_all | solution.py:68
  66.5 0.0 copy-start.6
  66.5 5.8 %all-to-all-start.1 = ((bf16[32,128,1024]{2,1,0:T(8,128)(2,1)}), bf16[32,128,1024]{2,1,0:T(8,128)(2,1)}, u32[]{:S(2)}, u32[]{:S(2)}) async-start(bf16[32,128,1024]{2,1,0:T(8,128)(2,1)} %bitcast.31), calls=%async_computation.1 | async-start | bytes 16777216 | tf_op jit(solution)/shard_map/all_to_all | solution.py:46
  72.3 0.0 all-gather.5.cloned.1.call-start
  72.3 0.7 all-gather.5.cloned.1.call-update
  73.0 0.0 all-gather.7.cloned.1.call-start
  73.1 96.8 %all-gather.5.cloned.1.call-done = bf16[1024,1024]{1,0:T(8,128)(2,1)} async-done(((bf16[128,1024]{1,0:T(8,128)(2,1)}), bf16[1024,1024]{1,0:T(8,128)(2,1)}) %all-gather.5.cloned.1.call-update) | async-done | bytes 2097168 | tf_op jit(solution)/shard_map/all_gather | solution.py:18
  169.8 0.0 all-gather.7.cloned.1.call-update
  169.8 0.0 copy-start.3
  169.8 0.2 all-gather.9.cloned.1.call-start
  170.1 0.0 copy-done.6
  170.1 0.6 pad_clamp_fusion
  170.7 0.7 gather_fusion
  171.4 0.9 gather_fusion.1
  172.2 3.4 %fusion.12 = bf16[32,512,128]{1,2,0:T(8,128)(2,1)} fusion(bf16[32,128,128]{2,1,0:T(8,128)(2,1)S(1)} %gather_fusion.1, s32[32,128]{1,0:T(8,128)S(1)} %gather_fusion), kind=kOutput, calls=%fused_computation.17 | convolution fusion | flops 541065216 | bytes 5259264 | tf_op jit(solution)/shard_map/stc,scr->rst/dot_general | solution.py:73
  175.6 101.1 %all-to-all-done.1 = bf16[32,128,1024]{2,1,0:T(8,128)(2,1)} async-done(((bf16[32,128,1024]{2,1,0:T(8,128)(2,1)}), bf16[32,128,1024]{2,1,0:T(8,128)(2,1)}, u32[]{:S(2)}, u32[]{:S(2)}) %all-to-all-start.1) | async-done | bytes 8388640 | tf_op jit(solution)/shard_map/all_to_all | solution.py:46
  276.7 0.0 copy-done.3
  276.7 5.7 %fusion.32 = f32[4096,128]{1,0:T(8,128)S(1)} fusion(bf16[4096,1024]{1,0:T(8,128)(2,1)} %bitcast.10, bf16[128,1024]{1,0:T(8,128)(2,1)S(1)} %copy-done.3), kind=kOutput, calls=%fused_computation.48 | convolution fusion | flops 1073741824 | bytes 10747904 | tf_op jit(solution)/shard_map/dot_general | solution.py:54
  282.4 0.0 copy-start.5
  282.4 2.1 copy.51
  284.5 0.0 copy-done.5
  284.5 8.4 %select_reduce_fusion = f32[128,128]{1,0:T(8,128)S(1)} fusion(f32[128,32,128]{2,1,0:T(8,128)} %copy.51, s32[128,128]{1,0:T(8,128)S(1)} %copy-done.5, s32[128,128]{1,0:T(8,128)S(1)} %get-tuple-element.3), kind=kOutput, calls=%fused_computation.18 | convolution fusion | flops 808960000 | bytes 2293760 | tf_op jit(solution)/shard_map/tpc,toc->tpo/dot_general | solution.py:58
  292.9 0.7 concatenate.3
  293.7 0.0 all-gather.9.cloned.1.call-update
  293.7 2.8 all-gather.7.cloned.1.call-done
  296.5 10.2 %convolution_convert_fusion = bf16[512,1024]{1,0:T(8,128)(2,1)} fusion(bf16[512,4096]{0,1:T(8,128)(2,1)} %bitcast.40, bf16[4096,1024]{1,0:T(8,128)(2,1)} %all-gather.7.cloned.1.call-done), kind=kOutput, calls=%fused_computation.21 | convolution fusion | flops 4295491584 | bytes 13631488 | tf_op jit(solution)/shard_map/dot_general | solution.py:75
  306.7 0.0 copy-done.2
  306.7 5.6 %fusion.17 = bf16[128,1024]{1,0:T(8,128)(2,1)} fusion(bf16[32,128,1024]{2,1,0:T(8,128)(2,1)} %all-to-all-done.1, bf16[128,32,128]{2,1,0:T(8,128)(2,1)S(1)} %copy-done.2), kind=kOutput, calls=%fused_computation.24 | convolution fusion | flops 1073872896 | bytes 9699328 | tf_op jit(solution)/shard_map/dot_general | solution.py:51
  312.3 13.4 %all-gather.9.cloned.1.call-done = f32[512,512]{1,0:T(8,128)} async-done(((f32[128,512]{1,0:T(8,128)}), f32[512,512]{1,0:T(8,128)}) %all-gather.9.cloned.1.call-update) | async-done | bytes 1048592 | tf_op jit(solution)/shard_map/all_gather | solution.py:65
  325.7 1.0 slice_reduce_fusion
  326.7 0.1 copy.52
  326.7 0.7 fusion.22
  (1 shorter events, 0.0 us)
Async XLA Ops:
  7.2 31.8 %copy-start = (bf16[512,1024]{1,0:T(8,128)(2,1)S(1)}, bf16[512,1024]{1,0:T(8,128)(2,1)}, u32[]{:S(2)}) copy-start(bf16[512,1024]{1,0:T(8,128)(2,1)} %param.7) | copy-start | bytes 3145732
  7.2 22.0 %all-to-all-start = ((s32[32,1,128]{2,1,0:T(1,128)}), s32[32,1,128]{2,1,0:T(1,128)S(1)}, u32[]{:S(2)}, u32[]{:S(2)}) async-start(s32[32,1,128]{2,1,0:T(1,128)} %bitcast.39), calls=%async_computation | async-start | bytes 32768 | tf_op jit(solution)/shard_map/all_to_all | solution.py:40
  21.0 8.3 %copy-start.4 = (s32[128,128]{1,0:T(8,128)}, s32[128,128]{1,0:T(8,128)S(1)}, u32[]{:S(2)}) copy-start(s32[128,128]{1,0:T(8,128)S(1)} %get-tuple-element.4) | copy-start | bytes 196612
  26.8 1.0 copy-start.1
  29.2 37.3 %all-to-all-start.2 = ((bf16[32,128,128]{2,1,0:T(8,128)(2,1)}), bf16[32,128,128]{2,1,0:T(8,128)(2,1)S(1)}, u32[]{:S(2)}, u32[]{:S(2)}) async-start(bf16[32,128,128]{2,1,0:T(8,128)(2,1)} %copy.50), calls=%async_computation.2 | async-start | bytes 2097152 | tf_op jit(solution)/shard_map/all_to_all | solution.py:68
  66.5 103.6 %copy-start.6 = (s32[32]{0:T(128)S(1)}, s32[32]{0:T(128)}, u32[]{:S(2)}) copy-start(s32[32]{0:T(128)} %constant.49) | copy-start | bytes 388
  66.5 210.2 %all-to-all-start.1 = ((bf16[32,128,1024]{2,1,0:T(8,128)(2,1)}), bf16[32,128,1024]{2,1,0:T(8,128)(2,1)}, u32[]{:S(2)}, u32[]{:S(2)}) async-start(bf16[32,128,1024]{2,1,0:T(8,128)(2,1)} %bitcast.31), calls=%async_computation.1 | async-start | bytes 16777216 | tf_op jit(solution)/shard_map/all_to_all | solution.py:46
  72.3 97.5 %all-gather.5.cloned.1.call-start = ((), (), s32[]{:S(2)}) async-start(), calls=%async_computation.3 | async-start | bytes 2359296 | tf_op jit(solution)/shard_map/all_gather | solution.py:18
  73.0 223.5 %all-gather.7.cloned.1.call-start = ((), (), s32[]{:S(2)}) async-start(), calls=%async_computation.4 | async-start | bytes 10485760 | tf_op jit(solution)/shard_map/all_gather | solution.py:19
  169.8 106.9 %copy-start.3 = (bf16[128,1024]{1,0:T(8,128)(2,1)S(1)}, bf16[128,1024]{1,0:T(8,128)(2,1)}, u32[]{:S(2)}) copy-start(bf16[128,1024]{1,0:T(8,128)(2,1)} %param.8) | copy-start | bytes 786436
  169.8 155.8 %all-gather.9.cloned.1.call-start = ((), (), s32[]{:S(2)}) async-start(), calls=%async_computation.5 | async-start | bytes 1310720 | tf_op jit(solution)/shard_map/all_gather | solution.py:65
  282.4 2.1 copy-start.5
  296.5 10.2 %copy-start.2 = (bf16[128,32,128]{2,1,0:T(8,128)(2,1)S(1)}, bf16[128,32,128]{2,1,0:T(8,128)(2,1)}, u32[]{:S(2)}) copy-start(bf16[128,32,128]{2,1,0:T(8,128)(2,1)} %copy-done.1) | copy-start | bytes 3145732
Sparse Core Ops, SparseCore 0:
  74.9 94.8 all-gather.4
  171.6 124.8 all-gather.6
  298.3 27.3 all-gather.8

commit v7 on v6

--- a/solution.py
+++ b/solution.py
@@ -56,7 +56,10 @@
     )
     products = products.reshape(tokens_here, owners, cap_slots)
     picked = jnp.einsum(
-        "tpc,toc->tpo", place_hot, products, precision=highest, preferred_element_type=jnp.float32
+        "tpc,toc->tpo",
+        place_hot.astype(jnp.bfloat16),
+        products.astype(jnp.bfloat16),
+        preferred_element_type=jnp.float32,
     )
     partial_dots = jnp.sum(picked * owner_hot, axis=-1).reshape(weights.shape)
     flat_dots = partial_dots.reshape(tokens_here, -1)

time: 335 us -> 334 us (level)
  transfers between devices with their start and end apart: 6 -> 6, of which waited for: 5 -> 5; matrix products, arithmetic and copies ran while one was open for 16% -> 17% of each run, Pallas kernels for 0% -> 0%
where the time goes in v7:
time: 334 us; the launch traced here: 333 us
  waiting for transfers between devices  235 us (70%)
  matrix products  44.6 us (13%)
  starting transfers between devices  27.4 us (8%)
  between operations  13.9 us (4%)
  local copies, waits for them, and re-layouts  8.22 us (2%)
  other arithmetic  3.9 us (1%)
    all_to_all x1, waiting for transfers between devices, body(): lax.all_to_all(looked.reshape(owners, cap_slots, width), MEM, 0, 0, tiled...  97.9 us
    all_gather x1, waiting for transfers between devices, body(): along_z = lax.all_gather(cotangent, 'mz', axis=0, tiled=True)  96.8 us
    all_to_all x1, waiting for transfers between devices, body(): lax.all_to_all(jnp.swapaxes(combined, 0, 1), MEM, 0, 0, tiled=True)  20.7 us
    all_gather x1, waiting for transfers between devices, body(): gathered = lax.all_gather(padded, 'pipe', axis=0)[:, :, :flat_dots.shape[1]]  13.5 us
    all_to_all x1, starting transfers between devices, body(): lax.all_to_all(row_lists[0], MEM, split_axis=0, concat_axis=0, tiled=True)  11.7 us
    dot_general x1, matrix products, body(): jnp.dot(in_rows.reshape(table_rows, slot_count), all_cot, preferred_eleme...  10.1 us
    all_to_all x1, starting transfers between devices, body(): lax.all_to_all(jnp.swapaxes(combined, 0, 1), MEM, 0, 0, tiled=True)  9.78 us
    dot_general x1, matrix products, body(): jnp.dot(row_hot.reshape(slot_count, table_rows), values, preferred_elemen...  6.77 us
  transfers between devices with their start and end apart: 6, of which 5 were waited for; matrix products, arithmetic and copies ran while one was open for 17% of the time, Pallas kernels for 0%

profile of v7, /device:TPU:6, one launch (start us, length us, event | category | flops | bytes accessed | tf_op | source)
XLA Modules:
  0.0 332.8 jit_solution(11332470216906802284)
XLA Ops:
  7.2 0.0 copy-start
  7.2 11.7 %all-to-all-start = ((s32[32,1,128]{2,1,0:T(1,128)}), s32[32,1,128]{2,1,0:T(1,128)S(1)}, u32[]{:S(2)}, u32[]{:S(2)}) async-start(s32[32,1,128]{2,1,0:T(1,128)} %bitcast.39), calls=%async_computation | async-start | bytes 32768 | tf_op jit(solution)/shard_map/all_to_all | solution.py:40
  18.9 1.0 fusion.19
  19.8 0.1 copy.48
  19.9 0.9 copy.44
  20.9 0.1 add_select_fusion.1
  21.0 0.0 copy-start.2
  21.0 5.9 %fusion.14 = bf16[128,32,128]{2,1,0:T(8,128)(2,1)S(1)} fusion(s32[128,128]{1,0:T(8,128)S(1)} %get-tuple-element.4, f32[128,128]{1,0:T(8,128)S(1)} %copy.48, s32[128,128]{1,0:T(8,128)S(1)} %get-tuple-element.3), kind=kOutput, calls=%fused_computation.24 | convolution fusion | flops 808976384 | bytes 1245184 | tf_op jit(solution)/shard_map/tpo,tpc->toc/dot_general | solution.py:33
  26.8 1.4 copy.50
  28.2 0.0 copy-done.2
  28.2 0.0 all-to-all-done
  28.2 9.8 %all-to-all-start.2 = ((bf16[32,128,128]{2,1,0:T(8,128)(2,1)}), bf16[32,128,128]{2,1,0:T(8,128)(2,1)S(1)}, u32[]{:S(2)}, u32[]{:S(2)}) async-start(bf16[32,128,128]{2,1,0:T(8,128)(2,1)} %copy.50), calls=%async_computation.2 | async-start | bytes 2097152 | tf_op jit(solution)/shard_map/all_to_all | solution.py:71
  38.0 0.0 copy-done
  38.0 6.8 %fusion.6 = bf16[4096,1024]{1,0:T(8,128)(2,1)} fusion(bf16[512,1024]{1,0:T(8,128)(2,1)S(1)} %copy-done, s32[4096]{0:T(1024)S(1)} %bitcast.32), kind=kOutput, calls=%fused_computation.12 | convolution fusion | flops 4301258752 | bytes 9453568 | tf_op jit(solution)/shard_map/dot_general | solution.py:43
  44.8 20.7 %all-to-all-done.2 = bf16[32,128,128]{2,1,0:T(8,128)(2,1)S(1)} async-done(((bf16[32,128,128]{2,1,0:T(8,128)(2,1)}), bf16[32,128,128]{2,1,0:T(8,128)(2,1)S(1)}, u32[]{:S(2)}, u32[]{:S(2)}) %all-to-all-start.2) | async-done | bytes 1048608 | tf_op jit(solution)/shard_map/all_to_all | solution.py:71
  65.5 5.6 %all-to-all-start.1 = ((bf16[32,128,1024]{2,1,0:T(8,128)(2,1)}), bf16[32,128,1024]{2,1,0:T(8,128)(2,1)}, u32[]{:S(2)}, u32[]{:S(2)}) async-start(bf16[32,128,1024]{2,1,0:T(8,128)(2,1)} %bitcast.30), calls=%async_computation.1 | async-start | bytes 16777216 | tf_op jit(solution)/shard_map/all_to_all | solution.py:46
  71.1 0.0 all-gather.5.cloned.1.call-start
  71.2 0.7 all-gather.5.cloned.1.call-update
  71.9 0.0 all-gather.7.cloned.1.call-start
  71.9 96.8 %all-gather.5.cloned.1.call-done = bf16[1024,1024]{1,0:T(8,128)(2,1)} async-done(((bf16[128,1024]{1,0:T(8,128)(2,1)}), bf16[1024,1024]{1,0:T(8,128)(2,1)}) %all-gather.5.cloned.1.call-update) | async-done | bytes 2097168 | tf_op jit(solution)/shard_map/all_gather | solution.py:18
  168.7 0.0 all-gather.7.cloned.1.call-update
  168.7 0.0 copy-start.1
  168.7 0.2 all-gather.9.cloned.1.call-start
  168.9 1.3 pad_clamp_fusion
  170.2 1.3 gather_fusion
  171.5 1.8 gather_fusion.1
  173.3 4.4 %fusion.12 = bf16[32,512,128]{1,2,0:T(8,128)(2,1)} fusion(bf16[32,128,128]{2,1,0:T(8,128)(2,1)} %gather_fusion.1, s32[32,128]{1,0:T(8,128)} %gather_fusion), kind=kOutput, calls=%fused_computation.19 | convolution fusion | flops 541065216 | bytes 5259264 | tf_op jit(solution)/shard_map/stc,scr->rst/dot_general | solution.py:76
  177.7 97.9 %all-to-all-done.1 = bf16[32,128,1024]{2,1,0:T(8,128)(2,1)} async-done(((bf16[32,128,1024]{2,1,0:T(8,128)(2,1)}), bf16[32,128,1024]{2,1,0:T(8,128)(2,1)}, u32[]{:S(2)}, u32[]{:S(2)}) %all-to-all-start.1) | async-done | bytes 8388640 | tf_op jit(solution)/shard_map/all_to_all | solution.py:46
  275.6 0.0 copy-done.1
  275.6 6.7 %convolution_convert_fusion = bf16[4096,128]{1,0:T(8,128)(2,1)} fusion(bf16[4096,1024]{1,0:T(8,128)(2,1)} %bitcast.10, bf16[128,1024]{1,0:T(8,128)(2,1)S(1)} %copy-done.1), kind=kOutput, calls=%fused_computation.13 | convolution fusion | flops 1074266112 | bytes 9699328 | tf_op jit(solution)/shard_map/dot_general | solution.py:54
  282.3 1.9 copy.51
  284.2 5.2 %select_reduce_fusion = f32[128,128]{1,0:T(8,128)S(1)} fusion(bf16[128,32,128]{2,1,0:T(8,128)(2,1)S(1)} %copy.51, s32[128,128]{1,0:T(8,128)} %copy-done.2, s32[128,128]{1,0:T(8,128)S(1)} %get-tuple-element.3), kind=kOutput, calls=%fused_computation.20 | convolution fusion | flops 142065664 | bytes 1245184 | tf_op jit(solution)/shard_map/tpc,toc->tpo/dot_general | solution.py:58
  289.4 0.7 concatenate.3
  290.1 0.0 all-gather.9.cloned.1.call-update
  290.1 5.2 %all-gather.7.cloned.1.call-done = bf16[4096,1024]{1,0:T(8,128)(2,1)} async-done(((bf16[1024,1024]{1,0:T(8,128)(2,1)}), bf16[4096,1024]{1,0:T(8,128)(2,1)}) %all-gather.7.cloned.1.call-update) | async-done | bytes 8388624 | tf_op jit(solution)/shard_map/all_gather | solution.py:19
  295.4 10.1 %convolution_convert_fusion.1 = bf16[512,1024]{1,0:T(8,128)(2,1)} fusion(bf16[512,4096]{0,1:T(8,128)(2,1)} %bitcast.40, bf16[4096,1024]{1,0:T(8,128)(2,1)} %all-gather.7.cloned.1.call-done), kind=kOutput, calls=%fused_computation.23 | convolution fusion | flops 4295491584 | bytes 13631488 | tf_op jit(solution)/shard_map/dot_general | solution.py:78
  305.5 5.6 %fusion.17 = bf16[128,1024]{1,0:T(8,128)(2,1)} fusion(bf16[32,128,1024]{2,1,0:T(8,128)(2,1)} %all-to-all-done.1, bf16[128,32,128]{2,1,0:T(8,128)(2,1)S(1)} %fusion.14), kind=kOutput, calls=%fused_computation.26 | convolution fusion | flops 1073872896 | bytes 9699328 | tf_op jit(solution)/shard_map/dot_general | solution.py:51
  311.1 13.5 %all-gather.9.cloned.1.call-done = f32[512,512]{1,0:T(8,128)} async-done(((f32[128,512]{1,0:T(8,128)}), f32[512,512]{1,0:T(8,128)}) %all-gather.9.cloned.1.call-update) | async-done | bytes 1048592 | tf_op jit(solution)/shard_map/all_gather | solution.py:68
  324.6 1.0 slice_reduce_fusion
  325.5 0.1 copy.52
  325.6 0.7 fusion.22
Async XLA Ops:
  7.2 30.9 %copy-start = (bf16[512,1024]{1,0:T(8,128)(2,1)S(1)}, bf16[512,1024]{1,0:T(8,128)(2,1)}, u32[]{:S(2)}) copy-start(bf16[512,1024]{1,0:T(8,128)(2,1)} %param.7) | copy-start | bytes 3145732
  7.2 21.1 %all-to-all-start = ((s32[32,1,128]{2,1,0:T(1,128)}), s32[32,1,128]{2,1,0:T(1,128)S(1)}, u32[]{:S(2)}, u32[]{:S(2)}) async-start(s32[32,1,128]{2,1,0:T(1,128)} %bitcast.39), calls=%async_computation | async-start | bytes 32768 | tf_op jit(solution)/shard_map/all_to_all | solution.py:40
  21.0 7.3 %copy-start.2 = (s32[128,128]{1,0:T(8,128)}, s32[128,128]{1,0:T(8,128)S(1)}, u32[]{:S(2)}) copy-start(s32[128,128]{1,0:T(8,128)S(1)} %get-tuple-element.4) | copy-start | bytes 196612
  28.2 37.3 %all-to-all-start.2 = ((bf16[32,128,128]{2,1,0:T(8,128)(2,1)}), bf16[32,128,128]{2,1,0:T(8,128)(2,1)S(1)}, u32[]{:S(2)}, u32[]{:S(2)}) async-start(bf16[32,128,128]{2,1,0:T(8,128)(2,1)} %copy.50), calls=%async_computation.2 | async-start | bytes 2097152 | tf_op jit(solution)/shard_map/all_to_all | solution.py:71
  65.5 210.1 %all-to-all-start.1 = ((bf16[32,128,1024]{2,1,0:T(8,128)(2,1)}), bf16[32,128,1024]{2,1,0:T(8,128)(2,1)}, u32[]{:S(2)}, u32[]{:S(2)}) async-start(bf16[32,128,1024]{2,1,0:T(8,128)(2,1)} %bitcast.30), calls=%async_computation.1 | async-start | bytes 16777216 | tf_op jit(solution)/shard_map/all_to_all | solution.py:46
  71.1 97.5 %all-gather.5.cloned.1.call-start = ((), (), s32[]{:S(2)}) async-start(), calls=%async_computation.3 | async-start | bytes 2359296 | tf_op jit(solution)/shard_map/all_gather | solution.py:18
  71.9 223.5 %all-gather.7.cloned.1.call-start = ((), (), s32[]{:S(2)}) async-start(), calls=%async_computation.4 | async-start | bytes 10485760 | tf_op jit(solution)/shard_map/all_gather | solution.py:19
  168.7 106.9 %copy-start.1 = (bf16[128,1024]{1,0:T(8,128)(2,1)S(1)}, bf16[128,1024]{1,0:T(8,128)(2,1)}, u32[]{:S(2)}) copy-start(bf16[128,1024]{1,0:T(8,128)(2,1)} %param.8) | copy-start | bytes 786436
  168.7 155.8 %all-gather.9.cloned.1.call-start = ((), (), s32[]{:S(2)}) async-start(), calls=%async_computation.5 | async-start | bytes 1310720 | tf_op jit(solution)/shard_map/all_gather | solution.py:68
Sparse Core Ops, SparseCore 0:
  73.7 94.8 all-gather.4
  170.5 124.8 all-gather.6
  297.2 27.3 all-gather.8
